TPU v7x, 128 devices: a whole 4x4x4 slice. The times are simulated.
128 devices in a mesh: sub: 128 (over z, y, x, core).
Axes of the slice: x: 4, y: 4, z: 4, core: 2. Of those that a mesh axis runs over, the one named last changes fastest.
Arguments:
- pool_inputs: bfloat16 [65536, 4096], P('sub'), may hold values from -6 to 6
- pool_targets: bfloat16 [65536, 4096], P('sub'), may hold values from -6 to 6
- row_picks: int32 [8, 32768], P(None, 'sub'), may hold values from 0 to 511
- weight_in: float32 [4096, 32768], P(None, 'sub'), may hold values from -6 to 6
- weight_out: float32 [4096, 32768], P(None, 'sub'), may hold values from -6 to 6
- eval_inputs: bfloat16 [256, 4096], P('sub'), may hold values from -6 to 6
- handover: int32 [4096], replicated, may hold values from 0 to 4095, as said below
Outputs:
- trained_in: float32 [4096, 32768], P(None, 'sub')
- trained_out: float32 [4096, 32768], P(None, 'sub')
- prediction: float32 [256, 4096], P('sub')
Inputs may be any that keep to these rules, and one draw needn't show every extreme that they name: `row_picks`: indices into the subnet's own 512 resident rows. handover[g] is the new position of neuron group g (neurons 8 g to 8 g + 7); every position is taken once, and no two groups of one subnet move to the same subnet.
All inputs are finite; a program needn't handle non-finite values.
Results may differ from a plain program's by a relative error of at most 0.0065.
Values may be sent and summed in bfloat16 or wider, within the bound.
No kernel may reach another device: no remote copies, remote signals or barrier semaphores. Data moves between devices by JAX's collectives and lax.ppermute only.
A program may use at most 192 MiB of HBM per device.

v0:
```python
import math

import jax
import jax.numpy as jnp
from jax import lax
from jax.experimental import pallas as pl
from jax.experimental.pallas import tpu as pltpu
from jax.sharding import PartitionSpec as P

D = 4096
GROUP = 8
STEPS = 4


tanh_coef = 0.7978845608028654
cubic_coef = 0.044715
step_rate = 0.5


def gelu_value(inputs):
    inner_term = tanh_coef * (inputs + cubic_coef * inputs * inputs * inputs)
    return 0.5 * inputs * (1.0 + jnp.tanh(inner_term))


def gelu_parts(inputs):
    tanh_part = jnp.tanh(tanh_coef * (inputs + cubic_coef * inputs * inputs * inputs))
    values = 0.5 * inputs * (1.0 + tanh_part)
    slopes = 0.5 * (1.0 + tanh_part) + 0.5 * inputs * (1.0 - tanh_part * tanh_part) * tanh_coef * (
        1.0 + 3.0 * cubic_coef * inputs * inputs
    )
    return (values, slopes)


NT = (((1,), (1,)), ((), ()))


def train_steps(scale_in, scale_out, picks_ref, pin_ref, ptg_ref, wi_ref, wo_ref, rows_ref):
    batch = picks_ref.shape[0]
    pool = pin_ref.shape[0]
    turns = picks_ref.shape[1]

    def one_turn(turn, carry):
        lanes = lax.broadcasted_iota(jnp.int32, (batch, turns), 1)
        picked = jnp.sum(jnp.where(lanes == turn, picks_ref[...], 0), axis=1, keepdims=True)
        onehot = (picked == lax.broadcasted_iota(jnp.int32, (batch, pool), 1)).astype(jnp.bfloat16)
        rows = jnp.dot(onehot, pin_ref[...], preferred_element_type=jnp.float32).astype(jnp.bfloat16)
        rows_ref[...] = rows
        in_half = wi_ref[...].astype(jnp.bfloat16)
        before = lax.dot_general(rows, in_half, NT, preferred_element_type=jnp.float32) * scale_in
        values, slopes = gelu_parts(before)
        activity = values.astype(jnp.bfloat16)
        activity_t = values.T.astype(jnp.bfloat16)
        goals = jnp.dot(onehot, ptg_ref[...], preferred_element_type=jnp.float32)
        out_half = wo_ref[...].astype(jnp.bfloat16)
        branch = jnp.dot(activity, out_half, preferred_element_type=jnp.float32) * scale_out
        errors = (branch - goals).astype(jnp.bfloat16)
        back = lax.dot_general(errors, out_half, NT, preferred_element_type=jnp.float32)
        grad_out = jnp.dot(activity_t, errors, preferred_element_type=jnp.float32) * scale_out
        wo_ref[...] = wo_ref[...] - step_rate * grad_out
        backward = back * scale_out * slopes
        backward_t = backward.astype(jnp.bfloat16).astype(jnp.float32).T.astype(jnp.bfloat16)
        grad_in = jnp.dot(backward_t, rows_ref[...], preferred_element_type=jnp.float32) * scale_in
        wi_ref[...] = wi_ref[...] - step_rate * grad_in
        return carry

    lax.fori_loop(0, turns, one_turn, 0)


def first_body(scale_in, scale_out, dest_ref, picks_ref, pin_ref, ptg_ref, wi0_ref, wo0_ref,
               inh_ref, outh_ref, send_ref, wi_ref, wo_ref, rows_ref, stage_ref, sems):
    wi_ref[...] = wi0_ref[...].T
    wo_ref[...] = wo0_ref[...].T
    train_steps(scale_in, scale_out, picks_ref, pin_ref, ptg_ref, wi_ref, wo_ref, rows_ref)
    inh_ref[...] = wi_ref[...].astype(jnp.bfloat16)
    outh_ref[...] = wo_ref[...].astype(jnp.bfloat16)
    groups = stage_ref.shape[0]

    def pack(g, carry):
        part = pl.ds(pl.multiple_of(g * GROUP, GROUP), GROUP)
        stage_ref[g] = jnp.concatenate([wi_ref[part, :], wo_ref[part, :]], axis=0).astype(jnp.bfloat16)
        return carry

    lax.fori_loop(0, groups, pack, 0)

    def send(g, carry):
        pltpu.make_async_copy(stage_ref.at[g], send_ref.at[dest_ref[g]], sems.at[g]).start()
        return carry

    lax.fori_loop(0, groups, send, 0)

    def finish(g, carry):
        pltpu.make_async_copy(stage_ref.at[g], send_ref.at[dest_ref[g]], sems.at[g]).wait()
        return carry

    lax.fori_loop(0, groups, finish, 0)


def second_body(scale_in, scale_out, src_ref, picks_ref, pin_ref, ptg_ref, land_ref,
                ti_ref, to_ref, wi_ref, wo_ref, rows_ref, stage_ref, sems):
    groups = stage_ref.shape[0]

    def fetch(g, carry):
        pltpu.make_async_copy(land_ref.at[src_ref[g]], stage_ref.at[g], sems.at[g]).start()
        return carry

    lax.fori_loop(0, groups, fetch, 0)

    def unpack(g, carry):
        pltpu.make_async_copy(land_ref.at[src_ref[g]], stage_ref.at[g], sems.at[g]).wait()
        block = stage_ref[g].astype(jnp.float32)
        part = pl.ds(pl.multiple_of(g * GROUP, GROUP), GROUP)
        wi_ref[part, :] = block[:GROUP]
        wo_ref[part, :] = block[GROUP:]
        return carry

    lax.fori_loop(0, groups, unpack, 0)
    train_steps(scale_in, scale_out, picks_ref, pin_ref, ptg_ref, wi_ref, wo_ref, rows_ref)
    ti_ref[...] = wi_ref[...].T
    to_ref[...] = wo_ref[...].T


def round_cost(hidden, width, batch, turns, pool):
    flops = turns * 2 * (2 * batch * pool * width + 5 * batch * hidden * width)
    return pl.CostEstimate(
        flops=flops,
        transcendentals=turns * batch * hidden,
        bytes_accessed=4 * hidden * width * 4 + 2 * pool * width * 2,
    )


VMEM_LIMIT = 63 * 1024 * 1024


def first_round(dests, picks_t, pool_inputs, pool_targets, weight_in, weight_out, owners, scale_in, scale_out):
    width, hidden = weight_in.shape
    batch, turns = picks_t.shape
    pool = pool_inputs.shape[0]
    groups = hidden // GROUP
    vmem = pl.BlockSpec(memory_space=pltpu.VMEM)
    return pl.pallas_call(
        lambda *refs: first_body(scale_in, scale_out, *refs),
        out_shape=(
            jax.ShapeDtypeStruct((hidden, width), jnp.bfloat16),
            jax.ShapeDtypeStruct((hidden, width), jnp.bfloat16),
            jax.ShapeDtypeStruct((owners, 2 * GROUP, width), jnp.bfloat16),
        ),
        in_specs=[pl.BlockSpec(memory_space=pltpu.SMEM)] + [vmem] * 5,
        out_specs=(vmem, vmem, pl.BlockSpec(memory_space=pl.ANY)),
        scratch_shapes=[
            pltpu.VMEM((hidden, width), jnp.float32),
            pltpu.VMEM((hidden, width), jnp.float32),
            pltpu.VMEM((batch, width), jnp.bfloat16),
            pltpu.VMEM((groups, 2 * GROUP, width), jnp.bfloat16),
            pltpu.SemaphoreType.DMA((groups,)),
        ],
        compiler_params=pltpu.CompilerParams(vmem_limit_bytes=VMEM_LIMIT),
        cost_estimate=round_cost(hidden, width, batch, turns, pool),
        name="first_round",
    )(dests, picks_t, pool_inputs, pool_targets, weight_in, weight_out)


def second_round(sources, picks_t, pool_inputs, pool_targets, landed, hidden, scale_in, scale_out):
    owners, _, width = landed.shape
    batch, turns = picks_t.shape
    pool = pool_inputs.shape[0]
    groups = hidden // GROUP
    vmem = pl.BlockSpec(memory_space=pltpu.VMEM)
    return pl.pallas_call(
        lambda *refs: second_body(scale_in, scale_out, *refs),
        out_shape=(
            jax.ShapeDtypeStruct((width, hidden), jnp.float32),
            jax.ShapeDtypeStruct((width, hidden), jnp.float32),
        ),
        in_specs=[pl.BlockSpec(memory_space=pltpu.SMEM), vmem, vmem, vmem,
                  pl.BlockSpec(memory_space=pl.ANY)],
        out_specs=(vmem, vmem),
        scratch_shapes=[
            pltpu.VMEM((hidden, width), jnp.float32),
            pltpu.VMEM((hidden, width), jnp.float32),
            pltpu.VMEM((batch, width), jnp.bfloat16),
            pltpu.VMEM((groups, 2 * GROUP, width), jnp.bfloat16),
            pltpu.SemaphoreType.DMA((groups,)),
        ],
        compiler_params=pltpu.CompilerParams(vmem_limit_bytes=VMEM_LIMIT),
        cost_estimate=round_cost(hidden, width, batch, turns, pool),
        name="second_round",
    )(sources, picks_t, pool_inputs, pool_targets, landed)


def per_device(pool_inputs, pool_targets, row_picks, weight_in, weight_out, eval_inputs, handover):
    owners = lax.axis_size("sub")
    my_index = lax.axis_index("sub")
    hidden = weight_in.shape[1]
    group_count = hidden // GROUP
    scale_in = 1.0 / math.sqrt(D)
    scale_out = 1.0 / math.sqrt(hidden * owners)
    eval_all = lax.all_to_all(
        jnp.broadcast_to(eval_inputs[None], (owners,) + eval_inputs.shape), "sub", 0, 0, tiled=True
    ).reshape(owners * eval_inputs.shape[0], eval_inputs.shape[1])
    picks_t = row_picks.T
    local_groups = lax.dynamic_slice_in_dim(handover, my_index * group_count, group_count, 0)
    dests = local_groups // group_count
    in_half, out_half, outgoing = first_round(
        dests, picks_t[:, :STEPS], pool_inputs, pool_targets, weight_in, weight_out, owners,
        scale_in, scale_out,
    )
    landed = lax.all_to_all(outgoing, "sub", 0, 0, tiled=True)
    in_half, out_half, landed = lax.optimization_barrier((in_half, out_half, landed))
    eval_act = gelu_value(
        lax.dot_general(eval_all, in_half, NT, preferred_element_type=jnp.float32) * scale_in
    ).astype(jnp.bfloat16)
    partial = jnp.dot(eval_act, out_half, preferred_element_type=jnp.float32) * scale_out
    rows_each = partial.shape[0] // owners
    parity = my_index % 2
    split = partial.reshape(owners // 2, 2, rows_each, partial.shape[1])
    mine = jnp.where(parity == 0, split[:, 0], split[:, 1])
    other = jnp.where(parity == 0, split[:, 1], split[:, 0])
    pairs = [(k, k ^ 1) for k in range(owners)]
    summed = mine + lax.ppermute(other, "sub", perm=pairs)
    same_parity = [list(range(0, owners, 2)), list(range(1, owners, 2))]
    gathered = lax.all_to_all(summed, "sub", 0, 0, tiled=True, axis_index_groups=same_parity)
    prediction = jnp.sum(gathered, axis=0)

    positions = my_index * group_count + jnp.arange(group_count, dtype=jnp.int32)
    arriving_match = handover[None, :] == positions[:, None]
    arriving = jnp.sum(
        jnp.where(arriving_match, jnp.arange(handover.shape[0], dtype=jnp.int32)[None, :], 0), axis=1
    )
    sources = arriving // group_count
    trained_in, trained_out = second_round(
        sources, picks_t[:, STEPS:], pool_inputs, pool_targets, landed, hidden, scale_in, scale_out
    )
    return (trained_in, trained_out, prediction)


def solution(mesh):
    in_specs = (
        P("sub", None),
        P("sub", None),
        P(None, "sub"),
        P(None, "sub"),
        P(None, "sub"),
        P("sub", None),
        P(),
    )
    out_specs = (P(None, "sub"), P(None, "sub"), P("sub", None))
    return jax.shard_map(
        per_device, mesh=mesh, in_specs=in_specs, out_specs=out_specs, check_vma=False
    )
```

profile of v0, /device:TPU:84, one launch (start us, length us, event | category | flops | bytes accessed | tf_op | source)
XLA Modules:
  0.0 372.5 jit_solution(16497756276126125609)
XLA Ops:
  0.6 4.1 %broadcast_in_dim.23 = bf16[128,2,4096]{2,1,0:T(2,128)(2,1)} broadcast(bf16[2,4096]{1,0:T(2,128)(2,1)} %param.12), dimensions={1,2} | broadcast | bytes 2113536 | tf_op jit(solution)/shard_map/broadcast_in_dim | solution.py:198
  4.8 10.4 %all-to-all-start.1 = ((bf16[128,2,4096]{2,1,0:T(2,128)(2,1)}), bf16[128,2,4096]{2,1,0:T(2,128)(2,1)}, u32[]{:S(2)}, u32[]{:S(2)}) async-start(bf16[128,2,4096]{2,1,0:T(2,128)(2,1)} %broadcast_in_dim.23), calls=%async_computation.1 | async-start | bytes 4194304 | tf_op jit(solution)/shard_map/all_to_all | solution.py:197
  15.2 0.0 copy-done.1
  15.2 0.6 and_select_fusion.refs_0_
  15.8 0.0 copy-done.2
  15.8 0.1 copy.15
  15.9 0.8 fusion.19
  16.6 35.4 %first_round.1 = (bf16[256,4096]{1,0:T(8,128)(2,1)}, bf16[256,4096]{1,0:T(8,128)(2,1)}, bf16[128,16,4096]{2,1,0:T(8,128)(2,1)}) custom-call(s32[32]{0:T(128)} %and_select_fusion.refs_0_, s32[256,4]{1,0:T(8,128)} %get-tuple-element.19.refs_1_, bf16[512,4096]{1,0:T(8,128)(2,1)} %refs_2_.3, bf16[512,4096]{1,0:T(8,128)(2,1)} %refs_3_.3, f32[4096,256]{1,0:T(8,128)} %refs_4_.1, ...), custom_call_target="tpu_custom_call" | custom-call | flops 19327352832 | bytes 25165824 | tf_op jit(solution)/shard_map/first_round/pallas_call | solution.py:140
  52.0 0.0 all-to-all-done.1
  52.0 10.2 %all-to-all-start = ((bf16[128,16,4096]{2,1,0:T(8,128)(2,1)}), bf16[128,16,4096]{2,1,0:T(8,128)(2,1)}, u32[]{:S(2)}, u32[]{:S(2)}) async-start(bf16[128,16,4096]{2,1,0:T(8,128)(2,1)} %get-tuple-element.13), calls=%async_computation | async-start | bytes 33554432 | tf_op jit(solution)/shard_map/all_to_all | solution.py:207
  62.3 2.7 reshape.22
  65.0 237.0 %all-to-all-done.refs_4_ = bf16[128,16,4096]{2,1,0:T(8,128)(2,1)} async-done(((bf16[128,16,4096]{2,1,0:T(8,128)(2,1)}), bf16[128,16,4096]{2,1,0:T(8,128)(2,1)}, u32[]{:S(2)}, u32[]{:S(2)}) %all-to-all-start) | async-done | bytes 16777248 | tf_op jit(solution)/shard_map/all_to_all | solution.py:207
  302.0 6.8 %convolution_multiply_fusion = f32[256,4096]{1,0:T(8,128)} fusion(bf16[256,4096]{1,0:T(8,128)(2,1)} %get-tuple-element.18, bf16[256,4096]{1,0:T(8,128)(2,1)} %get-tuple-element.17, bf16[256,4096]{1,0:T(8,128)(2,1)S(1)} %reshape.22), kind=kOutput, calls=%fused_computation | convolution fusion | flops 1075445760 | bytes 10485760 | tf_op jit(solution)/shard_map/dot_general | solution.py:212
  308.8 5.8 %reshape.23 = f32[64,2,2,4096]{3,2,1,0:T(2,128)} reshape(f32[256,4096]{1,0:T(8,128)} %convolution_multiply_fusion) | data formatting | bytes 8388608 | tf_op jit(solution)/shard_map/reshape | solution.py:215
  314.6 3.9 %fusion = f32[64,2,4096]{2,1,0:T(2,128)S(1)} fusion(pred[]{:T(512)S(6)} %eq.22, f32[64,2,2,4096]{3,2,1,0:T(2,128)} %reshape.23), kind=kLoop, calls=%fused_computation.2 | loop fusion | flops 524288 | bytes 6291457 | tf_op jit(solution)/shard_map/jit(_where)/select_n | solution.py:217
  318.5 0.1 collective-permute-start
  318.6 4.1 %collective-permute-done = f32[64,2,4096]{2,1,0:T(2,128)S(1)} collective-permute-done((f32[64,2,4096]{2,1,0:T(2,128)S(1)}, f32[64,2,4096]{2,1,0:T(2,128)S(1)}, u32[]{:S(2)}, u32[]{:S(2)}) %collective-permute-start) | collective-permute-done | bytes 2097184 | tf_op jit(solution)/shard_map/ppermute | solution.py:219
  322.8 3.1 fusion.2
  325.8 10.5 %all-to-all-start.2 = ((f32[64,2,4096]{2,1,0:T(2,128)}), f32[64,2,4096]{2,1,0:T(2,128)}, u32[]{:S(2)}, u32[]{:S(2)}) async-start(f32[64,2,4096]{2,1,0:T(2,128)} %fusion.2), calls=%async_computation.2 | async-start | bytes 4194304 | tf_op jit(solution)/shard_map/all_to_all | solution.py:221
  336.4 0.2 select_reduce_fusion
  336.6 0.5 and_select_fusion.1.refs_0_
  337.1 32.5 %second_round.1 = (f32[4096,256]{1,0:T(8,128)}, f32[4096,256]{1,0:T(8,128)}) custom-call(s32[32]{0:T(128)} %and_select_fusion.1.refs_0_, s32[256,4]{1,0:T(8,128)} %get-tuple-element.20.refs_1_, bf16[512,4096]{1,0:T(8,128)(2,1)} %refs_2_.3, bf16[512,4096]{1,0:T(8,128)(2,1)} %refs_3_.3, bf16[128,16,4096]{2,1,0:T(8,128)(2,1)} %all-to-all-done.refs_4_), custom_call_target="tpu_custom_call" | custom-call | flops 19327352832 | bytes 25165824 | tf_op jit(solution)/shard_map/second_round/pallas_call | solution.py:168
  369.6 0.0 all-to-all-done.2
  369.6 2.8 reduce_sum.19
  (5 shorter events, 0.0 us)
Async XLA Ops:
  4.8 10.4 %copy-start.1 = (s32[4096]{0:T(1024)S(1)}, s32[4096]{0:T(1024)}, u32[]{:S(2)}) copy-start(s32[4096]{0:T(1024)} %param.13) | copy-start | bytes 49156
  4.8 11.0 %copy-start.2 = (s32[8,256]{1,0:T(8,128)S(1)}, s32[8,256]{1,0:T(8,128)}, u32[]{:S(2)}) copy-start(s32[8,256]{1,0:T(8,128)} %param.9) | copy-start | bytes 24580
  4.8 47.3 %all-to-all-start.1 = ((bf16[128,2,4096]{2,1,0:T(2,128)(2,1)}), bf16[128,2,4096]{2,1,0:T(2,128)(2,1)}, u32[]{:S(2)}, u32[]{:S(2)}) async-start(bf16[128,2,4096]{2,1,0:T(2,128)(2,1)} %broadcast_in_dim.23), calls=%async_computation.1 | async-start | bytes 4194304 | tf_op jit(solution)/shard_map/all_to_all | solution.py:197
  52.0 250.0 %all-to-all-start = ((bf16[128,16,4096]{2,1,0:T(8,128)(2,1)}), bf16[128,16,4096]{2,1,0:T(8,128)(2,1)}, u32[]{:S(2)}, u32[]{:S(2)}) async-start(bf16[128,16,4096]{2,1,0:T(8,128)(2,1)} %get-tuple-element.13), calls=%async_computation | async-start | bytes 33554432 | tf_op jit(solution)/shard_map/all_to_all | solution.py:207
  314.6 8.1 %copy-start = (f32[64,2,2,4096]{3,2,1,0:T(2,128)S(1)}, f32[64,2,2,4096]{3,2,1,0:T(2,128)}, u32[]{:S(2)}) copy-start(f32[64,2,2,4096]{3,2,1,0:T(2,128)} %reshape.23) | copy-start | bytes 12582916
  318.5 4.2 %collective-permute-start = (f32[64,2,4096]{2,1,0:T(2,128)S(1)}, f32[64,2,4096]{2,1,0:T(2,128)S(1)}, u32[]{:S(2)}, u32[]{:S(2)}) collective-permute-start(f32[64,2,4096]{2,1,0:T(2,128)S(1)} %fusion), channel_id=1, source_target_pairs={{0,1},{1,0},{2,3},{3,2},{4,5},{5,4},{6,7},{7,6},{8,9},{9,8},{10,11... | collective-permute-start | bytes 6291464 | tf_op jit(solution)/shard_map/ppermute | solution.py:219
  325.8 43.8 %all-to-all-start.2 = ((f32[64,2,4096]{2,1,0:T(2,128)}), f32[64,2,4096]{2,1,0:T(2,128)}, u32[]{:S(2)}, u32[]{:S(2)}) async-start(f32[64,2,4096]{2,1,0:T(2,128)} %fusion.2), calls=%async_computation.2 | async-start | bytes 4194304 | tf_op jit(solution)/shard_map/all_to_all | solution.py:221
where the time goes:
time: 375 us; the launch traced here: 372 us
  waiting for transfers between devices  241 us (64%)
  Pallas kernels  67.9 us (18%)
  starting transfers between devices  31.2 us (8%)
  local copies, waits for them, and re-layouts  13.6 us (4%)
  other arithmetic  11.2 us (3%)
  matrix products  6.77 us (2%)
    all_to_all x1, waiting for transfers between devices, per_device(): landed = lax.all_to_all(outgoing, 'sub', 0, 0, tiled=True)  237 us
    pallas_call x1, Pallas kernels, first_round(): pl.pallas_call(lambda *refs: first_body(scale_in, scale_out, *refs), out_...  35.4 us
    pallas_call x1, Pallas kernels, second_round(): pl.pallas_call(lambda *refs: second_body(scale_in, scale_out, *refs), out...  32.5 us
    all_to_all x1, starting transfers between devices, per_device(): lax.all_to_all(summed, 'sub', 0, 0, tiled=True, axis_index_groups=same_pa...  10.5 us
    all_to_all x1, starting transfers between devices, per_device(): lax.all_to_all(jnp.broadcast_to(eval_inputs[None], (owners,) + eval_input...  10.4 us
    all_to_all x1, starting transfers between devices, per_device(): landed = lax.all_to_all(outgoing, 'sub', 0, 0, tiled=True)  10.2 us
  transfers between devices with their start and end apart: 4, of which 2 were waited for; matrix products, arithmetic and copies ran while one was open for 1% of the time, Pallas kernels for 18%

commit v1 on v0

--- a/solution.py
+++ b/solution.py
@@ -194,9 +194,13 @@
     group_count = hidden // GROUP
     scale_in = 1.0 / math.sqrt(D)
     scale_out = 1.0 / math.sqrt(hidden * owners)
-    eval_all = lax.all_to_all(
-        jnp.broadcast_to(eval_inputs[None], (owners,) + eval_inputs.shape), "sub", 0, 0, tiled=True
-    ).reshape(owners * eval_inputs.shape[0], eval_inputs.shape[1])
+    eval_rows = eval_inputs.shape[0]
+    eval_all = (
+        lax.all_gather(eval_inputs, "sub", axis=0, tiled=True)
+        .reshape(owners // 2, 2, eval_rows, D)
+        .transpose(1, 0, 2, 3)
+        .reshape(owners * eval_rows, D)
+    )
     picks_t = row_picks.T
     local_groups = lax.dynamic_slice_in_dim(handover, my_index * group_count, group_count, 0)
     dests = local_groups // group_count
@@ -212,9 +216,13 @@
     partial = jnp.dot(eval_act, out_half, preferred_element_type=jnp.float32) * scale_out
     rows_each = partial.shape[0] // owners
     parity = my_index % 2
-    split = partial.reshape(owners // 2, 2, rows_each, partial.shape[1])
-    mine = jnp.where(parity == 0, split[:, 0], split[:, 1])
-    other = jnp.where(parity == 0, split[:, 1], split[:, 0])
+    half = partial.shape[0] // 2
+    mine = lax.dynamic_slice_in_dim(partial, parity * half, half, 0).reshape(
+        owners // 2, rows_each, partial.shape[1]
+    )
+    other = lax.dynamic_slice_in_dim(partial, (1 - parity) * half, half, 0).reshape(
+        owners // 2, rows_each, partial.shape[1]
+    )
     pairs = [(k, k ^ 1) for k in range(owners)]
     summed = mine + lax.ppermute(other, "sub", perm=pairs)
     same_parity = [list(range(0, owners, 2)), list(range(1, owners, 2))]

time: 375 us -> 381 us (1.016)
  between operations: 0.76 us -> 14.1 us
  starting transfers between devices: 31.2 us -> 21.3 us
  local copies, waits for them, and re-layouts: 13.6 us -> 19.3 us
    all_to_all x1, waiting for transfers between devices: 237 us -> 7.5 us  [per_device(): landed = lax.all_to_all(outgoing, 'sub', 0, 0, tiled=True)]
    all_gather x0 -> x1, waiting for transfers between devices: none -> 228 us  [per_device(): lax.all_gather(eval_inputs, 'sub', axis=0, tiled=True)]
    all_to_all x1 -> x0, starting transfers between devices: 10.4 us -> none  [per_device(): lax.all_to_all(jnp.broadcast_to(eval_inputs[None], (owners,) + eval_input...]
    reshape x2 -> x4, local copies, waits for them, and re-layouts: 8.56 us -> 13.8 us  [the longest x2 8.02 us: per_device(): eval_all = lax.all_gather(eval_inputs, 'sub', axis=0, tiled=True).reshape...]
    broadcast_in_dim x1 -> x0, local copies, waits for them, and re-layouts: 4.13 us -> none  [per_device(): jnp.broadcast_to(eval_inputs[None], (owners,) + eval_inputs.shape)]
    dynamic_slice x0 -> x1, local copies, waits for them, and re-layouts: none -> 3.92 us  [per_device(): lax.dynamic_slice_in_dim(partial, (1 - parity) * half, half, 0)]
    select_n x1 -> x0, other arithmetic: 3.89 us -> none  [per_device(): other = jnp.where(parity == 0, split[:, 1], split[:, 0])]
  transfers between devices with their start and end apart: 4 -> 4, of which waited for: 2 -> 3; matrix products, arithmetic and copies ran while one was open for 1% -> 3% of each run, Pallas kernels for 18% -> 9%
where the time goes in v1:
time: 381 us; the launch traced here: 378 us
  waiting for transfers between devices  238 us (62%)
  Pallas kernels  67.8 us (18%)
  starting transfers between devices  21.3 us (6%)
  local copies, waits for them, and re-layouts  19.3 us (5%)
  between operations  14.1 us (4%)
  other arithmetic  10.6 us (3%)
  matrix products  6.77 us (2%)
    all_gather x1, waiting for transfers between devices, per_device(): lax.all_gather(eval_inputs, 'sub', axis=0, tiled=True)  228 us
    pallas_call x1, Pallas kernels, first_round(): pl.pallas_call(lambda *refs: first_body(scale_in, scale_out, *refs), out_...  35.3 us
    pallas_call x1, Pallas kernels, second_round(): pl.pallas_call(lambda *refs: second_body(scale_in, scale_out, *refs), out...  32.5 us
    all_to_all x1, starting transfers between devices, per_device(): lax.all_to_all(summed, 'sub', 0, 0, tiled=True, axis_index_groups=same_pa...  10.7 us
    all_to_all x1, starting transfers between devices, per_device(): landed = lax.all_to_all(outgoing, 'sub', 0, 0, tiled=True)  10.4 us
    reshape x2, local copies, waits for them, and re-layouts, per_device(): eval_all = lax.all_gather(eval_inputs, 'sub', axis=0, tiled=True).reshape...  8.02 us
  transfers between devices with their start and end apart: 4, of which 3 were waited for; matrix products, arithmetic and copies ran while one was open for 3% of the time, Pallas kernels for 9%

profile of v1, /device:TPU:84, one launch (start us, length us, event | category | flops | bytes accessed | tf_op | source)
XLA Modules:
  0.0 378.2 jit_solution(3398714340837240226)
XLA Ops:
  7.2 0.8 copy.15
  8.0 0.8 fusion.16
  8.7 1.3 and_select_fusion.refs_0_
  10.0 35.3 %first_round.1 = (bf16[256,4096]{1,0:T(8,128)(2,1)}, bf16[256,4096]{1,0:T(8,128)(2,1)}, bf16[128,16,4096]{2,1,0:T(8,128)(2,1)}) custom-call(s32[32]{0:T(128)} %and_select_fusion.refs_0_, s32[256,4]{1,0:T(8,128)} %get-tuple-element.21.refs_1_, bf16[512,4096]{1,0:T(8,128)(2,1)} %refs_2_.3, bf16[512,4096]{1,0:T(8,128)(2,1)} %refs_3_.3, f32[4096,256]{1,0:T(8,128)} %refs_4_.1, ...), custom_call_target="tpu_custom_call" | custom-call | flops 19327352832 | bytes 25165824 | tf_op jit(solution)/shard_map/first_round/pallas_call | solution.py:140
  45.3 10.4 %all-to-all-start = ((bf16[128,16,4096]{2,1,0:T(8,128)(2,1)}), bf16[128,16,4096]{2,1,0:T(8,128)(2,1)}, u32[]{:S(2)}, u32[]{:S(2)}) async-start(bf16[128,16,4096]{2,1,0:T(8,128)(2,1)} %get-tuple-element.13), calls=%async_computation | async-start | bytes 33554432 | tf_op jit(solution)/shard_map/all_to_all | solution.py:211
  55.7 0.2 all-gather.3.cloned.1.call-start
  55.9 0.5 all-gather.3.cloned.1.call-update
  56.4 228.2 %all-gather.3.cloned.1.call-done = bf16[128,2,4096]{2,1,0:T(2,128)(2,1)} async-done(((bf16[1,2,4096]{2,1,0:T(2,128)(2,1)}), bf16[128,2,4096]{2,1,0:T(2,128)(2,1)}) %all-gather.3.cloned.1.call-update) | async-done | bytes 2097168 | tf_op jit(solution)/shard_map/all_gather | solution.py:199
  284.7 5.3 %copy.18 = bf16[64,2,2,4096]{3,2,0,1:T(2,128)(2,1)} copy(bf16[64,2,2,4096]{3,2,1,0:T(2,128)(2,1)} %bitcast.19) | data formatting | bytes 4194304 | tf_op jit(solution)/shard_map/reshape | solution.py:200
  289.9 2.7 reshape.24
  292.7 7.5 %all-to-all-done.refs_4_ = bf16[128,16,4096]{2,1,0:T(8,128)(2,1)} async-done(((bf16[128,16,4096]{2,1,0:T(8,128)(2,1)}), bf16[128,16,4096]{2,1,0:T(8,128)(2,1)}, u32[]{:S(2)}, u32[]{:S(2)}) %all-to-all-start) | async-done | bytes 16777248 | tf_op jit(solution)/shard_map/all_to_all | solution.py:211
  300.2 6.8 %convolution_multiply_fusion = f32[256,4096]{1,0:T(8,128)} fusion(bf16[256,4096]{1,0:T(8,128)(2,1)} %get-tuple-element.18, bf16[256,4096]{1,0:T(8,128)(2,1)} %get-tuple-element.17, bf16[256,4096]{1,0:T(8,128)(2,1)S(1)} %reshape.24), kind=kOutput, calls=%fused_computation | convolution fusion | flops 1075445760 | bytes 10485760 | tf_op jit(solution)/shard_map/dot_general | solution.py:216
  307.0 3.9 %constant_dynamic-slice_fusion.1 = (f32[128,4096]{1,0:T(8,128)}, f32[128,4096]{1,0:T(8,128)S(1)}) fusion(f32[256,4096]{1,0:T(8,128)} %convolution_multiply_fusion, s32[]{:T(128)S(6)} %select_n.34, s32[]{:T(128)S(6)} %select_n.33), kind=kLoop, calls=%fused_computation.23 | loop fusion | bytes 8388616 | tf_op jit(solution)/shard_map/dynamic_slice | solution.py:223
  310.9 3.5 reshape.26
  314.4 0.0 collective-permute-start
  314.4 2.2 reshape.25
  316.6 2.3 collective-permute-done
  318.9 5.7 %add.46 = f32[64,2,4096]{2,1,0:T(2,128)} add(f32[64,2,4096]{2,1,0:T(2,128)} %reshape.25, f32[64,2,4096]{2,1,0:T(2,128)} %collective-permute-done) | non-fusion elementwise | flops 524288 | bytes 6291456 | tf_op jit(solution)/shard_map/add | solution.py:227
  324.6 10.7 %all-to-all-start.1 = ((f32[64,2,4096]{2,1,0:T(2,128)}), f32[64,2,4096]{2,1,0:T(2,128)}, u32[]{:S(2)}, u32[]{:S(2)}) async-start(f32[64,2,4096]{2,1,0:T(2,128)} %add.46), calls=%async_computation.1 | async-start | bytes 4194304 | tf_op jit(solution)/shard_map/all_to_all | solution.py:229
  335.3 0.2 select_reduce_fusion
  335.5 0.5 and_select_fusion.1.refs_0_
  336.1 32.5 %second_round.1 = (f32[4096,256]{1,0:T(8,128)}, f32[4096,256]{1,0:T(8,128)}) custom-call(s32[32]{0:T(128)} %and_select_fusion.1.refs_0_, s32[256,4]{1,0:T(8,128)} %get-tuple-element.22.refs_1_, bf16[512,4096]{1,0:T(8,128)(2,1)} %refs_2_.3, bf16[512,4096]{1,0:T(8,128)(2,1)} %refs_3_.3, bf16[128,16,4096]{2,1,0:T(8,128)(2,1)} %all-to-all-done.refs_4_), custom_call_target="tpu_custom_call" | custom-call | flops 19327352832 | bytes 25165824 | tf_op jit(solution)/shard_map/second_round/pallas_call | solution.py:168
  368.5 0.0 all-to-all-done.1
  368.6 2.8 reduce_sum.19
  (3 shorter events, 0.0 us)
Async XLA Ops:
  45.3 254.9 %all-to-all-start = ((bf16[128,16,4096]{2,1,0:T(8,128)(2,1)}), bf16[128,16,4096]{2,1,0:T(8,128)(2,1)}, u32[]{:S(2)}, u32[]{:S(2)}) async-start(bf16[128,16,4096]{2,1,0:T(8,128)(2,1)} %get-tuple-element.13), calls=%async_computation | async-start | bytes 33554432 | tf_op jit(solution)/shard_map/all_to_all | solution.py:211
  55.7 229.0 %all-gather.3.cloned.1.call-start = ((), (), s32[]{:S(2)}) async-start(), calls=%async_computation.2 | async-start | bytes 2113536 | tf_op jit(solution)/shard_map/all_gather | solution.py:199
  314.4 4.5 %collective-permute-start = (f32[64,2,4096]{2,1,0:T(2,128)}, f32[64,2,4096]{2,1,0:T(2,128)}, u32[]{:S(2)}, u32[]{:S(2)}) collective-permute-start(f32[64,2,4096]{2,1,0:T(2,128)} %reshape.26), channel_id=1, source_target_pairs={{0,1},{1,0},{2,3},{3,2},{4,5},{5,4},{6,7},{7,6},{8,9},{9,8},{10,11... | collective-permute-start | bytes 6291464 | tf_op jit(solution)/shard_map/ppermute | solution.py:227
  324.6 10.7 %copy-start = (s32[4096]{0:T(1024)S(1)}, s32[4096]{0:T(1024)}, u32[]{:S(2)}) copy-start(s32[4096]{0:T(1024)} %param.13) | copy-start | bytes 49156
  324.6 44.0 %all-to-all-start.1 = ((f32[64,2,4096]{2,1,0:T(2,128)}), f32[64,2,4096]{2,1,0:T(2,128)}, u32[]{:S(2)}, u32[]{:S(2)}) async-start(f32[64,2,4096]{2,1,0:T(2,128)} %add.46), calls=%async_computation.1 | async-start | bytes 4194304 | tf_op jit(solution)/shard_map/all_to_all | solution.py:229
Sparse Core Ops, SparseCore 0:
  59.7 224.9 all-gather.2

commit v2 on v0

--- a/solution.py
+++ b/solution.py
@@ -205,7 +205,6 @@
         scale_in, scale_out,
     )
     landed = lax.all_to_all(outgoing, "sub", 0, 0, tiled=True)
-    in_half, out_half, landed = lax.optimization_barrier((in_half, out_half, landed))
     eval_act = gelu_value(
         lax.dot_general(eval_all, in_half, NT, preferred_element_type=jnp.float32) * scale_in
     ).astype(jnp.bfloat16)
@@ -215,6 +214,7 @@
     split = partial.reshape(owners // 2, 2, rows_each, partial.shape[1])
     mine = jnp.where(parity == 0, split[:, 0], split[:, 1])
     other = jnp.where(parity == 0, split[:, 1], split[:, 0])
+    mine, other, landed = lax.optimization_barrier((mine, other, landed))
     pairs = [(k, k ^ 1) for k in range(owners)]
     summed = mine + lax.ppermute(other, "sub", perm=pairs)
     same_parity = [list(range(0, owners, 2)), list(range(1, owners, 2))]

time: 375 us -> 358 us (0.955)
  waiting for transfers between devices: 241 us -> 222 us
    all_to_all x1, waiting for transfers between devices: 237 us -> 218 us  [per_device(): landed = lax.all_to_all(outgoing, 'sub', 0, 0, tiled=True)]
    select_n x0 -> x1, other arithmetic: none -> 3.89 us  [per_device(): mine = jnp.where(parity == 0, split[:, 0], split[:, 1])]
  transfers between devices with their start and end apart: 4 -> 4, of which waited for: 2 -> 2; matrix products, arithmetic and copies ran while one was open for 1% -> 7% of each run, Pallas kernels for 18% -> 19%
where the time goes in v2:
time: 358 us; the launch traced here: 356 us
  waiting for transfers between devices  222 us (62%)
  Pallas kernels  67.8 us (19%)
  starting transfers between devices  31.2 us (9%)
  other arithmetic  13.7 us (4%)
  local copies, waits for them, and re-layouts  13.6 us (4%)
  matrix products  6.78 us (2%)
    all_to_all x1, waiting for transfers between devices, per_device(): landed = lax.all_to_all(outgoing, 'sub', 0, 0, tiled=True)  218 us
    pallas_call x1, Pallas kernels, first_round(): pl.pallas_call(lambda *refs: first_body(scale_in, scale_out, *refs), out_...  35.3 us
    pallas_call x1, Pallas kernels, second_round(): pl.pallas_call(lambda *refs: second_body(scale_in, scale_out, *refs), out...  32.5 us
    all_to_all x1, starting transfers between devices, per_device(): lax.all_to_all(summed, 'sub', 0, 0, tiled=True, axis_index_groups=same_pa...  10.5 us
    all_to_all x1, starting transfers between devices, per_device(): lax.all_to_all(jnp.broadcast_to(eval_inputs[None], (owners,) + eval_input...  10.4 us
    all_to_all x1, starting transfers between devices, per_device(): landed = lax.all_to_all(outgoing, 'sub', 0, 0, tiled=True)  10.2 us
  transfers between devices with their start and end apart: 4, of which 2 were waited for; matrix products, arithmetic and copies ran while one was open for 7% of the time, Pallas kernels for 19%

profile of v2, /device:TPU:84, one launch (start us, length us, event | category | flops | bytes accessed | tf_op | source)
XLA Modules:
  0.0 355.8 jit_solution(4902172110169379663)
XLA Ops:
  0.6 4.1 %broadcast_in_dim.23 = bf16[128,2,4096]{2,1,0:T(2,128)(2,1)} broadcast(bf16[2,4096]{1,0:T(2,128)(2,1)} %param.12), dimensions={1,2} | broadcast | bytes 2113536 | tf_op jit(solution)/shard_map/broadcast_in_dim | solution.py:198
  4.8 10.4 %all-to-all-start = ((bf16[128,2,4096]{2,1,0:T(2,128)(2,1)}), bf16[128,2,4096]{2,1,0:T(2,128)(2,1)}, u32[]{:S(2)}, u32[]{:S(2)}) async-start(bf16[128,2,4096]{2,1,0:T(2,128)(2,1)} %broadcast_in_dim.23), calls=%async_computation | async-start | bytes 4194304 | tf_op jit(solution)/shard_map/all_to_all | solution.py:197
  15.2 0.0 copy-done.1
  15.2 0.6 and_select_fusion.refs_0_
  15.8 0.1 copy.15
  15.9 0.8 fusion.18
  16.6 35.3 %first_round.1 = (bf16[256,4096]{1,0:T(8,128)(2,1)}, bf16[256,4096]{1,0:T(8,128)(2,1)}, bf16[128,16,4096]{2,1,0:T(8,128)(2,1)}) custom-call(s32[32]{0:T(128)} %and_select_fusion.refs_0_, s32[256,4]{1,0:T(8,128)} %get-tuple-element.19.refs_1_, bf16[512,4096]{1,0:T(8,128)(2,1)} %refs_2_.3, bf16[512,4096]{1,0:T(8,128)(2,1)} %refs_3_.3, f32[4096,256]{1,0:T(8,128)} %refs_4_.1, ...), custom_call_target="tpu_custom_call" | custom-call | flops 19327352832 | bytes 25165824 | tf_op jit(solution)/shard_map/first_round/pallas_call | solution.py:140
  52.0 0.0 all-to-all-done
  52.0 10.2 %all-to-all-start.1 = ((bf16[128,16,4096]{2,1,0:T(8,128)(2,1)}), bf16[128,16,4096]{2,1,0:T(8,128)(2,1)}, u32[]{:S(2)}, u32[]{:S(2)}) async-start(bf16[128,16,4096]{2,1,0:T(8,128)(2,1)} %get-tuple-element.13), calls=%async_computation.1 | async-start | bytes 33554432 | tf_op jit(solution)/shard_map/all_to_all | solution.py:207
  62.2 2.7 reshape.22
  65.0 6.8 %convolution_multiply_fusion = f32[256,4096]{1,0:T(8,128)} fusion(bf16[256,4096]{1,0:T(8,128)(2,1)} %get-tuple-element.12, bf16[256,4096]{1,0:T(8,128)(2,1)} %get-tuple-element.11, bf16[256,4096]{1,0:T(8,128)(2,1)S(1)} %reshape.22), kind=kOutput, calls=%fused_computation | convolution fusion | flops 1075445760 | bytes 10485760 | tf_op jit(solution)/shard_map/dot_general | solution.py:211
  71.8 5.8 %reshape.23 = f32[64,2,2,4096]{3,2,1,0:T(2,128)} reshape(f32[256,4096]{1,0:T(8,128)} %convolution_multiply_fusion) | data formatting | bytes 8388608 | tf_op jit(solution)/shard_map/reshape | solution.py:214
  77.6 3.9 %fusion.1 = f32[64,2,4096]{2,1,0:T(2,128)S(1)} fusion(pred[]{:T(512)S(6)} %eq.22, f32[64,2,2,4096]{3,2,1,0:T(2,128)} %reshape.23), kind=kLoop, calls=%fused_computation.4 | loop fusion | flops 524288 | bytes 6291457 | tf_op jit(solution)/shard_map/jit(_where)/select_n | solution.py:215
  81.5 2.8 fusion
  84.3 217.7 %all-to-all-done.1.refs_4_ = bf16[128,16,4096]{2,1,0:T(8,128)(2,1)} async-done(((bf16[128,16,4096]{2,1,0:T(8,128)(2,1)}), bf16[128,16,4096]{2,1,0:T(8,128)(2,1)}, u32[]{:S(2)}, u32[]{:S(2)}) %all-to-all-start.1) | async-done | bytes 16777248 | tf_op jit(solution)/shard_map/all_to_all | solution.py:207
  302.0 0.0 collective-permute-start
  302.0 4.4 %collective-permute-done = f32[64,2,4096]{2,1,0:T(2,128)S(1)} collective-permute-done((f32[64,2,4096]{2,1,0:T(2,128)}, f32[64,2,4096]{2,1,0:T(2,128)S(1)}, u32[]{:S(2)}, u32[]{:S(2)}) %collective-permute-start) | collective-permute-done | bytes 2097184 | tf_op jit(solution)/shard_map/ppermute | solution.py:219
  306.3 2.8 add.38
  309.1 10.5 %all-to-all-start.2 = ((f32[64,2,4096]{2,1,0:T(2,128)}), f32[64,2,4096]{2,1,0:T(2,128)}, u32[]{:S(2)}, u32[]{:S(2)}) async-start(f32[64,2,4096]{2,1,0:T(2,128)} %add.38), calls=%async_computation.2 | async-start | bytes 4194304 | tf_op jit(solution)/shard_map/all_to_all | solution.py:221
  319.7 0.2 select_reduce_fusion
  319.9 0.5 and_select_fusion.1.refs_0_
  320.4 32.5 %second_round.1 = (f32[4096,256]{1,0:T(8,128)}, f32[4096,256]{1,0:T(8,128)}) custom-call(s32[32]{0:T(128)} %and_select_fusion.1.refs_0_, s32[256,4]{1,0:T(8,128)} %get-tuple-element.20.refs_1_, bf16[512,4096]{1,0:T(8,128)(2,1)} %refs_2_.3, bf16[512,4096]{1,0:T(8,128)(2,1)} %refs_3_.3, bf16[128,16,4096]{2,1,0:T(8,128)(2,1)} %all-to-all-done.1.refs_4_), custom_call_target="tpu_custom_call" | custom-call | flops 19327352832 | bytes 25165824 | tf_op jit(solution)/shard_map/second_round/pallas_call | solution.py:168
  352.9 0.0 all-to-all-done.2
  352.9 2.8 reduce_sum.19
  (6 shorter events, 0.0 us)
Async XLA Ops:
  4.8 10.4 %copy-start.1 = (s32[4096]{0:T(1024)S(1)}, s32[4096]{0:T(1024)}, u32[]{:S(2)}) copy-start(s32[4096]{0:T(1024)} %param.13) | copy-start | bytes 49156
  4.8 11.0 %copy-start.2 = (s32[8,256]{1,0:T(8,128)S(1)}, s32[8,256]{1,0:T(8,128)}, u32[]{:S(2)}) copy-start(s32[8,256]{1,0:T(8,128)} %param.9) | copy-start | bytes 24580
  4.8 47.2 %all-to-all-start = ((bf16[128,2,4096]{2,1,0:T(2,128)(2,1)}), bf16[128,2,4096]{2,1,0:T(2,128)(2,1)}, u32[]{:S(2)}, u32[]{:S(2)}) async-start(bf16[128,2,4096]{2,1,0:T(2,128)(2,1)} %broadcast_in_dim.23), calls=%async_computation | async-start | bytes 4194304 | tf_op jit(solution)/shard_map/all_to_all | solution.py:197
  52.0 250.0 %all-to-all-start.1 = ((bf16[128,16,4096]{2,1,0:T(8,128)(2,1)}), bf16[128,16,4096]{2,1,0:T(8,128)(2,1)}, u32[]{:S(2)}, u32[]{:S(2)}) async-start(bf16[128,16,4096]{2,1,0:T(8,128)(2,1)} %get-tuple-element.13), calls=%async_computation.1 | async-start | bytes 33554432 | tf_op jit(solution)/shard_map/all_to_all | solution.py:207
  77.6 3.9 %copy-start = (f32[64,2,2,4096]{3,2,1,0:T(2,128)S(1)}, f32[64,2,2,4096]{3,2,1,0:T(2,128)}, u32[]{:S(2)}) copy-start(f32[64,2,2,4096]{3,2,1,0:T(2,128)} %reshape.23) | copy-start | bytes 12582916
  302.0 4.4 %collective-permute-start = (f32[64,2,4096]{2,1,0:T(2,128)}, f32[64,2,4096]{2,1,0:T(2,128)S(1)}, u32[]{:S(2)}, u32[]{:S(2)}) collective-permute-start(f32[64,2,4096]{2,1,0:T(2,128)} %fusion), channel_id=1, source_target_pairs={{0,1},{1,0},{2,3},{3,2},{4,5},{5,4},{6,7},{7,6},{8,9},{9,8},{10,11... | collective-permute-start | bytes 6291464 | tf_op jit(solution)/shard_map/ppermute | solution.py:219
  309.1 43.8 %all-to-all-start.2 = ((f32[64,2,4096]{2,1,0:T(2,128)}), f32[64,2,4096]{2,1,0:T(2,128)}, u32[]{:S(2)}, u32[]{:S(2)}) async-start(f32[64,2,4096]{2,1,0:T(2,128)} %add.38), calls=%async_computation.2 | async-start | bytes 4194304 | tf_op jit(solution)/shard_map/all_to_all | solution.py:221

commit v3 on v2

--- a/solution.py
+++ b/solution.py
@@ -66,33 +66,13 @@
     lax.fori_loop(0, turns, one_turn, 0)
 
 
-def first_body(scale_in, scale_out, dest_ref, picks_ref, pin_ref, ptg_ref, wi0_ref, wo0_ref,
-               inh_ref, outh_ref, send_ref, wi_ref, wo_ref, rows_ref, stage_ref, sems):
+def first_body(scale_in, scale_out, picks_ref, pin_ref, ptg_ref, wi0_ref, wo0_ref,
+               inh_ref, outh_ref, wi_ref, wo_ref, rows_ref):
     wi_ref[...] = wi0_ref[...].T
     wo_ref[...] = wo0_ref[...].T
     train_steps(scale_in, scale_out, picks_ref, pin_ref, ptg_ref, wi_ref, wo_ref, rows_ref)
     inh_ref[...] = wi_ref[...].astype(jnp.bfloat16)
     outh_ref[...] = wo_ref[...].astype(jnp.bfloat16)
-    groups = stage_ref.shape[0]
-
-    def pack(g, carry):
-        part = pl.ds(pl.multiple_of(g * GROUP, GROUP), GROUP)
-        stage_ref[g] = jnp.concatenate([wi_ref[part, :], wo_ref[part, :]], axis=0).astype(jnp.bfloat16)
-        return carry
-
-    lax.fori_loop(0, groups, pack, 0)
-
-    def send(g, carry):
-        pltpu.make_async_copy(stage_ref.at[g], send_ref.at[dest_ref[g]], sems.at[g]).start()
-        return carry
-
-    lax.fori_loop(0, groups, send, 0)
-
-    def finish(g, carry):
-        pltpu.make_async_copy(stage_ref.at[g], send_ref.at[dest_ref[g]], sems.at[g]).wait()
-        return carry
-
-    lax.fori_loop(0, groups, finish, 0)
 
 
 def second_body(scale_in, scale_out, src_ref, picks_ref, pin_ref, ptg_ref, land_ref,
@@ -131,36 +111,32 @@
 VMEM_LIMIT = 63 * 1024 * 1024
 
 
-def first_round(dests, picks_t, pool_inputs, pool_targets, weight_in, weight_out, owners, scale_in, scale_out):
+def first_round(picks_t, pool_inputs, pool_targets, weight_in, weight_out, scale_in, scale_out):
     width, hidden = weight_in.shape
     batch, turns = picks_t.shape
     pool = pool_inputs.shape[0]
-    groups = hidden // GROUP
     vmem = pl.BlockSpec(memory_space=pltpu.VMEM)
     return pl.pallas_call(
         lambda *refs: first_body(scale_in, scale_out, *refs),
         out_shape=(
             jax.ShapeDtypeStruct((hidden, width), jnp.bfloat16),
             jax.ShapeDtypeStruct((hidden, width), jnp.bfloat16),
-            jax.ShapeDtypeStruct((owners, 2 * GROUP, width), jnp.bfloat16),
         ),
-        in_specs=[pl.BlockSpec(memory_space=pltpu.SMEM)] + [vmem] * 5,
-        out_specs=(vmem, vmem, pl.BlockSpec(memory_space=pl.ANY)),
+        in_specs=[vmem] * 5,
+        out_specs=(vmem, vmem),
         scratch_shapes=[
             pltpu.VMEM((hidden, width), jnp.float32),
             pltpu.VMEM((hidden, width), jnp.float32),
             pltpu.VMEM((batch, width), jnp.bfloat16),
-            pltpu.VMEM((groups, 2 * GROUP, width), jnp.bfloat16),
-            pltpu.SemaphoreType.DMA((groups,)),
         ],
         compiler_params=pltpu.CompilerParams(vmem_limit_bytes=VMEM_LIMIT),
         cost_estimate=round_cost(hidden, width, batch, turns, pool),
         name="first_round",
-    )(dests, picks_t, pool_inputs, pool_targets, weight_in, weight_out)
+    )(picks_t, pool_inputs, pool_targets, weight_in, weight_out)
 
 
 def second_round(sources, picks_t, pool_inputs, pool_targets, landed, hidden, scale_in, scale_out):
-    owners, _, width = landed.shape
+    _, _, width = landed.shape
     batch, turns = picks_t.shape
     pool = pool_inputs.shape[0]
     groups = hidden // GROUP
@@ -198,13 +174,34 @@
         jnp.broadcast_to(eval_inputs[None], (owners,) + eval_inputs.shape), "sub", 0, 0, tiled=True
     ).reshape(owners * eval_inputs.shape[0], eval_inputs.shape[1])
     picks_t = row_picks.T
-    local_groups = lax.dynamic_slice_in_dim(handover, my_index * group_count, group_count, 0)
-    dests = local_groups // group_count
-    in_half, out_half, outgoing = first_round(
-        dests, picks_t[:, :STEPS], pool_inputs, pool_targets, weight_in, weight_out, owners,
-        scale_in, scale_out,
-    )
-    landed = lax.all_to_all(outgoing, "sub", 0, 0, tiled=True)
+    in_half, out_half = first_round(
+        picks_t[:, :STEPS], pool_inputs, pool_targets, weight_in, weight_out, scale_in, scale_out
+    )
+    pieces = owners
+    piece = 2 * GROUP * D // pieces
+    splits = pieces // (2 * GROUP)
+    stacked = jnp.concatenate(
+        [in_half.reshape(group_count, GROUP, D), out_half.reshape(group_count, GROUP, D)], axis=1
+    )
+    spread = (
+        stacked.reshape(group_count, 2 * GROUP, splits, piece)
+        .transpose(1, 2, 0, 3)
+        .reshape(pieces, group_count, piece)
+    )
+    held = lax.all_to_all(spread, "sub", 0, 0, tiled=True).reshape(owners * group_count, piece)
+    total_groups = owners * group_count
+    inverse = (
+        jnp.zeros((total_groups,), jnp.int32)
+        .at[handover]
+        .set(jnp.arange(total_groups, dtype=jnp.int32))
+    )
+    forward = jnp.take(held, inverse, axis=0).reshape(owners, group_count, piece)
+    arrived = lax.all_to_all(forward, "sub", 0, 0, tiled=True)
+    landed = (
+        arrived.reshape(2 * GROUP, splits, group_count, piece)
+        .transpose(2, 0, 1, 3)
+        .reshape(group_count, 2 * GROUP, D)
+    )
     eval_act = gelu_value(
         lax.dot_general(eval_all, in_half, NT, preferred_element_type=jnp.float32) * scale_in
     ).astype(jnp.bfloat16)
@@ -221,12 +218,7 @@
     gathered = lax.all_to_all(summed, "sub", 0, 0, tiled=True, axis_index_groups=same_parity)
     prediction = jnp.sum(gathered, axis=0)
 
-    positions = my_index * group_count + jnp.arange(group_count, dtype=jnp.int32)
-    arriving_match = handover[None, :] == positions[:, None]
-    arriving = jnp.sum(
-        jnp.where(arriving_match, jnp.arange(handover.shape[0], dtype=jnp.int32)[None, :], 0), axis=1
-    )
-    sources = arriving // group_count
+    sources = jnp.arange(group_count, dtype=jnp.int32)
     trained_in, trained_out = second_round(
         sources, picks_t[:, STEPS:], pool_inputs, pool_targets, landed, hidden, scale_in, scale_out
     )

time: 358 us -> 280 us (0.78)
  waiting for transfers between devices: 222 us -> 26.6 us
  local copies, waits for them, and re-layouts: 13.6 us -> 70.8 us
  blocking collectives: 0 us -> 56.7 us
  other arithmetic: 13.7 us -> 17.4 us
    all_to_all x1, waiting for transfers between devices: 218 us -> 22.2 us  [per_device(): arrived = lax.all_to_all(forward, 'sub', 0, 0, tiled=True)]
    all_to_all x0 -> x1, blocking collectives: none -> 56.7 us  [per_device(): lax.all_to_all(spread, 'sub', 0, 0, tiled=True)]
    gather x0 -> x1, local copies, waits for them, and re-layouts: none -> 20.2 us  [per_device(): jnp.take(held, inverse, axis=0).reshape(owners, group_count, piece)]
    scatter x0 -> x1, local copies, waits for them, and re-layouts: none -> 15.5 us  [per_device(): inverse = jnp.zeros((total_groups,), jnp.int32).at[handover].set(jnp.aran...]
    reshape x0 -> x1, local copies, waits for them, and re-layouts: none -> 7.4 us  [per_device(): landed = arrived.reshape(2 * GROUP, splits, group_count, piece).transpose...]
    all_to_all x0 -> x1, local copies, waits for them, and re-layouts: none -> 6.54 us  [per_device(): arrived = lax.all_to_all(forward, 'sub', 0, 0, tiled=True)]
    concatenate x0 -> x2, local copies, waits for them, and re-layouts: none -> 4.07 us  [per_device(): jnp.concatenate([in_half.reshape(group_count, GROUP, D), out_half.reshape...]
  transfers between devices with their start and end apart: 4 -> 4, of which waited for: 2 -> 2; matrix products, arithmetic and copies ran while one was open for 7% -> 23% of each run, Pallas kernels for 19% -> 12%
where the time goes in v3:
time: 280 us; the launch traced here: 277 us
  local copies, waits for them, and re-layouts  70.8 us (25%)
  Pallas kernels  64.7 us (23%)
  blocking collectives  56.7 us (20%)
  starting transfers between devices  32.9 us (12%)
  waiting for transfers between devices  26.6 us (10%)
  other arithmetic  17.4 us (6%)
  matrix products  6.77 us (2%)
    all_to_all x1, blocking collectives, per_device(): lax.all_to_all(spread, 'sub', 0, 0, tiled=True)  56.7 us
    pallas_call x1, Pallas kernels, second_round(): pl.pallas_call(lambda *refs: second_body(scale_in, scale_out, *refs), out...  32.5 us
    pallas_call x1, Pallas kernels, first_round(): pl.pallas_call(lambda *refs: first_body(scale_in, scale_out, *refs), out_...  32.2 us
    all_to_all x1, waiting for transfers between devices, per_device(): arrived = lax.all_to_all(forward, 'sub', 0, 0, tiled=True)  22.2 us
    gather x1, local copies, waits for them, and re-layouts, per_device(): jnp.take(held, inverse, axis=0).reshape(owners, group_count, piece)  20.2 us
    scatter x1, local copies, waits for them, and re-layouts, per_device(): inverse = jnp.zeros((total_groups,), jnp.int32).at[handover].set(jnp.aran...  15.5 us
    all_to_all x1, starting transfers between devices, per_device(): lax.all_to_all(summed, 'sub', 0, 0, tiled=True, axis_index_groups=same_pa...  11.7 us
    all_to_all x1, starting transfers between devices, per_device(): lax.all_to_all(jnp.broadcast_to(eval_inputs[None], (owners,) + eval_input...  10.9 us
  transfers between devices with their start and end apart: 4, of which 2 were waited for; matrix products, arithmetic and copies ran while one was open for 23% of the time, Pallas kernels for 12%

profile of v3, /device:TPU:84, one launch (start us, length us, event | category | flops | bytes accessed | tf_op | source)
XLA Modules:
  0.0 276.6 jit_solution(6339480312506082560)
XLA Ops:
  2.2 32.2 %first_round.1 = (bf16[256,4096]{1,0:T(8,128)(2,1)}, bf16[256,4096]{1,0:T(8,128)(2,1)}) custom-call(s32[256,4]{1,0:T(8,128)} %get-tuple-element.17.refs_0_, bf16[512,4096]{1,0:T(8,128)(2,1)} %refs_2_.3, bf16[512,4096]{1,0:T(8,128)(2,1)} %refs_3_.3, f32[4096,256]{1,0:T(8,128)} %refs_3_.2, f32[4096,256]{1,0:T(8,128)} %refs_4_.1), custom_call_target="tpu_custom_call" | custom-call | flops 19327352832 | bytes 25165824 | tf_op jit(solution)/shard_map/first_round/pallas_call | solution.py:119
  34.4 2.9 %copy.21 = bf16[32,8,8,512]{3,0,2,1:T(8,128)(2,1)S(1)} copy(bf16[32,8,8,512]{3,1,2,0:T(8,128)(2,1)} %bitcast.47) | data formatting | bytes 4194304 | tf_op jit(solution)/shard_map/concatenate | solution.py:183
  37.3 1.2 copy.22
  38.9 56.7 %all_to_all.20 = bf16[128,32,512]{2,1,0:T(8,128)(2,1)} all-to-all(bf16[128,32,512]{2,1,0:T(8,128)(2,1)S(1)} %bitcast.45), channel_id=1, replica_groups=mesh['sub'=128] {'sub'}, dimensions={0} | all-to-all | bytes 8388608 | tf_op jit(solution)/shard_map/all_to_all | solution.py:191
  95.6 3.4 %broadcast_in_dim.23 = bf16[128,2,4096]{2,1,0:T(2,128)(2,1)} broadcast(bf16[2,4096]{1,0:T(2,128)(2,1)S(1)} %copy-done.4), dimensions={1,2} | broadcast | bytes 2113536 | tf_op jit(solution)/shard_map/broadcast_in_dim | solution.py:174
  99.0 10.9 %all-to-all-start = ((bf16[128,2,4096]{2,1,0:T(2,128)(2,1)}), bf16[128,2,4096]{2,1,0:T(2,128)(2,1)S(1)}, u32[]{:S(2)}, u32[]{:S(2)}) async-start(bf16[128,2,4096]{2,1,0:T(2,128)(2,1)} %broadcast_in_dim.23), calls=%async_computation | async-start | bytes 4194304 | tf_op jit(solution)/shard_map/all_to_all | solution.py:173
  110.0 15.5 %scatter_custom_fusion = s32[4096]{0:T(1024)S(1)} fusion(s32[4096]{0:T(1024)S(1)} %compare_select_fusion.1, s32[4096]{0:T(1024)S(1)} %iota.7, s32[]{:T(128)} %constant.17.clone.1), kind=kCustom, calls=%fused_computation.25 | custom fusion | bytes 16388 | tf_op jit(solution)/shard_map/scatter | solution.py:196
  125.7 20.2 %gather_fusion = bf16[4096,512]{1,0:T(8,128)(2,1)} fusion(bf16[4096,512]{1,0:T(8,128)(2,1)} %bitcast.43, s32[4096]{0:T(1024)S(1)} %fusion.13), kind=kCustom, calls=%fused_computation | custom fusion | bytes 8404992 | tf_op jit(solution)/shard_map/jit(_take)/gather | solution.py:198
  145.8 3.9 %broadcast_select_fusion = bf16[128,32,512]{2,1,0:T(8,128)(2,1)} fusion(bf16[128,32,512]{2,1,0:T(8,128)(2,1)} %bitcast.44, pred[128,32]{1,0:T(8,128)(4,1)S(1)} %broadcast_in_dim.25), kind=kLoop, calls=%fused_computation.6 | loop fusion | flops 2097152 | bytes 8392704 | tf_op jit(solution)/shard_map/jit(_take)/select_n | solution.py:198
  149.8 1.3 copy-done.3
  151.1 10.2 %all-to-all-start.2 = ((bf16[128,32,512]{2,1,0:T(8,128)(2,1)}), bf16[128,32,512]{2,1,0:T(8,128)(2,1)}, u32[]{:S(2)}, u32[]{:S(2)}) async-start(bf16[128,32,512]{2,1,0:T(8,128)(2,1)} %broadcast_select_fusion), calls=%async_computation.2 | async-start | bytes 8388608 | tf_op jit(solution)/shard_map/all_to_all | solution.py:199
  161.4 4.3 %reshape.48 = bf16[256,4096]{1,0:T(8,128)(2,1)} reshape(bf16[128,2,4096]{2,1,0:T(2,128)(2,1)} %copy-done.3) | data formatting | bytes 4194304 | tf_op jit(solution)/shard_map/reshape | solution.py:175
  165.7 6.8 %convolution_multiply_fusion = f32[256,4096]{1,0:T(8,128)} fusion(bf16[256,4096]{1,0:T(8,128)(2,1)} %get-tuple-element.11, bf16[256,4096]{1,0:T(8,128)(2,1)S(1)} %copy-done.1, bf16[256,4096]{1,0:T(8,128)(2,1)} %reshape.48), kind=kOutput, calls=%fused_computation.2 | convolution fusion | flops 1075445760 | bytes 10485760 | tf_op jit(solution)/shard_map/dot_general | solution.py:208
  172.4 5.9 %reshape.49 = f32[64,2,2,4096]{3,2,1,0:T(2,128)} reshape(f32[256,4096]{1,0:T(8,128)} %convolution_multiply_fusion) | data formatting | bytes 8388608 | tf_op jit(solution)/shard_map/reshape | solution.py:211
  178.3 5.8 %fusion = f32[64,2,4096]{2,1,0:T(2,128)} fusion(pred[]{:T(512)S(6)} %eq.6, f32[64,2,2,4096]{3,2,1,0:T(2,128)} %reshape.49), kind=kLoop, calls=%fused_computation.7 | loop fusion | flops 524288 | bytes 6291457 | tf_op jit(solution)/shard_map/jit(_where)/select_n | solution.py:213
  184.2 1.5 fusion.1
  185.7 22.2 %all-to-all-done.2 = bf16[128,32,512]{2,1,0:T(8,128)(2,1)} async-done(((bf16[128,32,512]{2,1,0:T(8,128)(2,1)}), bf16[128,32,512]{2,1,0:T(8,128)(2,1)}, u32[]{:S(2)}, u32[]{:S(2)}) %all-to-all-start.2) | async-done | bytes 4194336 | tf_op jit(solution)/shard_map/all_to_all | solution.py:199
  207.9 6.5 %copy.26 = bf16[128,32,512]{2,0,1:T(8,128)(2,1)} copy(bf16[128,32,512]{2,1,0:T(8,128)(2,1)} %all-to-all-done.2) | data formatting | bytes 8388608 | tf_op jit(solution)/shard_map/all_to_all | solution.py:199
  214.4 7.4 %reshape.53.refs_4_ = bf16[32,16,4096]{2,1,0:T(8,128)(2,1)} reshape(bf16[32,16,8,512]{3,2,1,0:T(8,128)(2,1)} %bitcast.46) | data formatting | bytes 8388608 | tf_op jit(solution)/shard_map/reshape | solution.py:203
  221.8 4.4 %collective-permute-done = f32[64,2,4096]{2,1,0:T(2,128)S(1)} collective-permute-done((f32[64,2,4096]{2,1,0:T(2,128)}, f32[64,2,4096]{2,1,0:T(2,128)S(1)}, u32[]{:S(2)}, u32[]{:S(2)}) %collective-permute-start) | collective-permute-done | bytes 2097184 | tf_op jit(solution)/shard_map/ppermute | solution.py:216
  226.2 2.8 %add.35 = f32[64,2,4096]{2,1,0:T(2,128)} add(f32[64,2,4096]{2,1,0:T(2,128)S(1)} %fusion.1, f32[64,2,4096]{2,1,0:T(2,128)S(1)} %collective-permute-done) | non-fusion elementwise | flops 524288 | bytes 6291456 | tf_op jit(solution)/shard_map/add | solution.py:216
  229.0 11.7 %all-to-all-start.3 = ((f32[64,2,4096]{2,1,0:T(2,128)}), f32[64,2,4096]{2,1,0:T(2,128)}, u32[]{:S(2)}, u32[]{:S(2)}) async-start(f32[64,2,4096]{2,1,0:T(2,128)} %add.35), calls=%async_computation.3 | async-start | bytes 4194304 | tf_op jit(solution)/shard_map/all_to_all | solution.py:218
  241.3 32.5 %second_round.1 = (f32[4096,256]{1,0:T(8,128)}, f32[4096,256]{1,0:T(8,128)}) custom-call(s32[32]{0:T(128)} %iota.6.refs_0_, s32[256,4]{1,0:T(8,128)} %get-tuple-element.18.refs_1_, bf16[512,4096]{1,0:T(8,128)(2,1)} %refs_2_.3, bf16[512,4096]{1,0:T(8,128)(2,1)} %refs_3_.3, bf16[32,16,4096]{2,1,0:T(8,128)(2,1)} %reshape.53.refs_4_), custom_call_target="tpu_custom_call" | custom-call | flops 19327352832 | bytes 25165824 | tf_op jit(solution)/shard_map/second_round/pallas_call | solution.py:144
  273.8 2.8 %reduce_sum.9 = f32[2,4096]{1,0:T(2,128)} reduce(f32[64,2,4096]{2,1,0:T(2,128)} %all-to-all-done.3, f32[]{:T(128)} %constant.50.clone.1), dimensions={0}, to_apply=%region_1.2 | reduce | flops 516096 | bytes 2129924 | tf_op jit(solution)/shard_map/reduce_sum | solution.py:219
  (23 shorter events, 2.6 us)
Async XLA Ops:
  34.4 2.9 %copy-start.2 = (bf16[256,4096]{1,0:T(8,128)(2,1)S(1)}, bf16[256,4096]{1,0:T(8,128)(2,1)}, u32[]{:S(2)}) copy-start(bf16[256,4096]{1,0:T(8,128)(2,1)} %get-tuple-element.11) | copy-start | bytes 6291460
  38.9 56.7 %copy-start.4 = (bf16[2,4096]{1,0:T(2,128)(2,1)S(1)}, bf16[2,4096]{1,0:T(2,128)(2,1)}, u32[]{:S(2)}) copy-start(bf16[2,4096]{1,0:T(2,128)(2,1)} %param.12) | copy-start | bytes 49156
  99.0 11.0 %copy-start.5 = (s32[4096]{0:T(1024)S(1)}, s32[4096]{0:T(1024)}, u32[]{:S(2)}) copy-start(s32[4096]{0:T(1024)} %param.13) | copy-start | bytes 49156
  99.0 50.8 %all-to-all-start = ((bf16[128,2,4096]{2,1,0:T(2,128)(2,1)}), bf16[128,2,4096]{2,1,0:T(2,128)(2,1)S(1)}, u32[]{:S(2)}, u32[]{:S(2)}) async-start(bf16[128,2,4096]{2,1,0:T(2,128)(2,1)} %broadcast_in_dim.23), calls=%async_computation | async-start | bytes 4194304 | tf_op jit(solution)/shard_map/all_to_all | solution.py:173
  149.8 1.3 copy-start.3
  151.1 56.7 %all-to-all-start.2 = ((bf16[128,32,512]{2,1,0:T(8,128)(2,1)}), bf16[128,32,512]{2,1,0:T(8,128)(2,1)}, u32[]{:S(2)}, u32[]{:S(2)}) async-start(bf16[128,32,512]{2,1,0:T(8,128)(2,1)} %broadcast_select_fusion), calls=%async_computation.2 | async-start | bytes 8388608 | tf_op jit(solution)/shard_map/all_to_all | solution.py:199
  161.4 4.3 %copy-start.1 = (bf16[256,4096]{1,0:T(8,128)(2,1)S(1)}, bf16[256,4096]{1,0:T(8,128)(2,1)}, u32[]{:S(2)}) copy-start(bf16[256,4096]{1,0:T(8,128)(2,1)} %get-tuple-element.10) | copy-start | bytes 6291460
  178.3 5.8 %copy-start = (f32[64,2,2,4096]{3,2,1,0:T(2,128)S(1)}, f32[64,2,2,4096]{3,2,1,0:T(2,128)}, u32[]{:S(2)}) copy-start(f32[64,2,2,4096]{3,2,1,0:T(2,128)} %reshape.49) | copy-start | bytes 12582916
  221.8 4.4 %collective-permute-start = (f32[64,2,4096]{2,1,0:T(2,128)}, f32[64,2,4096]{2,1,0:T(2,128)S(1)}, u32[]{:S(2)}, u32[]{:S(2)}) collective-permute-start(f32[64,2,4096]{2,1,0:T(2,128)} %fusion), channel_id=1, source_target_pairs={{0,1},{1,0},{2,3},{3,2},{4,5},{5,4},{6,7},{7,6},{8,9},{9,8},{10,11... | collective-permute-start | bytes 6291464 | tf_op jit(solution)/shard_map/ppermute | solution.py:216
  229.0 44.7 %all-to-all-start.3 = ((f32[64,2,4096]{2,1,0:T(2,128)}), f32[64,2,4096]{2,1,0:T(2,128)}, u32[]{:S(2)}, u32[]{:S(2)}) async-start(f32[64,2,4096]{2,1,0:T(2,128)} %add.35), calls=%async_computation.3 | async-start | bytes 4194304 | tf_op jit(solution)/shard_map/all_to_all | solution.py:218

commit v4 on v3

--- a/solution.py
+++ b/solution.py
@@ -195,7 +195,9 @@
         .at[handover]
         .set(jnp.arange(total_groups, dtype=jnp.int32))
     )
-    forward = jnp.take(held, inverse, axis=0).reshape(owners, group_count, piece)
+    forward = jnp.take(held, inverse, axis=0, mode="clip").reshape(
+        owners, group_count, piece
+    )
     arrived = lax.all_to_all(forward, "sub", 0, 0, tiled=True)
     landed = (
         arrived.reshape(2 * GROUP, splits, group_count, piece)

time: 280 us -> 276 us (0.986)
  other arithmetic: 17.4 us -> 13.4 us
    select_n x1 -> x0, other arithmetic: 3.94 us -> none  [per_device(): jnp.take(held, inverse, axis=0).reshape(owners, group_count, piece)]
  transfers between devices with their start and end apart: 4 -> 4, of which waited for: 2 -> 2; matrix products, arithmetic and copies ran while one was open for 23% -> 22% of each run, Pallas kernels for 12% -> 12%
where the time goes in v4:
time: 276 us; the launch traced here: 273 us
  local copies, waits for them, and re-layouts  70.7 us (26%)
  Pallas kernels  64.7 us (23%)
  blocking collectives  56.7 us (21%)
  starting transfers between devices  32.9 us (12%)
  waiting for transfers between devices  26.6 us (10%)
  other arithmetic  13.4 us (5%)
  matrix products  6.77 us (2%)
    all_to_all x1, blocking collectives, per_device(): lax.all_to_all(spread, 'sub', 0, 0, tiled=True)  56.7 us
    pallas_call x1, Pallas kernels, second_round(): pl.pallas_call(lambda *refs: second_body(scale_in, scale_out, *refs), out...  32.5 us
    pallas_call x1, Pallas kernels, first_round(): pl.pallas_call(lambda *refs: first_body(scale_in, scale_out, *refs), out_...  32.2 us
    all_to_all x1, waiting for transfers between devices, per_device(): arrived = lax.all_to_all(forward, 'sub', 0, 0, tiled=True)  22.2 us
    gather x1, local copies, waits for them, and re-layouts, per_device(): jnp.take(held, inverse, axis=0, mode='clip')  20.2 us
    scatter x1, local copies, waits for them, and re-layouts, per_device(): inverse = jnp.zeros((total_groups,), jnp.int32).at[handover].set(jnp.aran...  15.5 us
    all_to_all x1, starting transfers between devices, per_device(): lax.all_to_all(summed, 'sub', 0, 0, tiled=True, axis_index_groups=same_pa...  11.7 us
    all_to_all x1, starting transfers between devices, per_device(): lax.all_to_all(jnp.broadcast_to(eval_inputs[None], (owners,) + eval_input...  10.9 us
  transfers between devices with their start and end apart: 4, of which 2 were waited for; matrix products, arithmetic and copies ran while one was open for 22% of the time, Pallas kernels for 12%

profile of v4, /device:TPU:84, one launch (start us, length us, event | category | flops | bytes accessed | tf_op | source)
XLA Modules:
  0.0 272.5 jit_solution(4518909906279103466)
XLA Ops:
  0.6 0.8 copy.16
  2.2 32.2 %first_round.1 = (bf16[256,4096]{1,0:T(8,128)(2,1)}, bf16[256,4096]{1,0:T(8,128)(2,1)}) custom-call(s32[256,4]{1,0:T(8,128)} %get-tuple-element.17.refs_0_, bf16[512,4096]{1,0:T(8,128)(2,1)} %refs_2_.3, bf16[512,4096]{1,0:T(8,128)(2,1)} %refs_3_.3, f32[4096,256]{1,0:T(8,128)} %refs_3_.2, f32[4096,256]{1,0:T(8,128)} %refs_4_.1), custom_call_target="tpu_custom_call" | custom-call | flops 19327352832 | bytes 25165824 | tf_op jit(solution)/shard_map/first_round/pallas_call | solution.py:119
  34.4 2.9 %copy.21 = bf16[32,8,8,512]{3,0,2,1:T(8,128)(2,1)S(1)} copy(bf16[32,8,8,512]{3,1,2,0:T(8,128)(2,1)} %bitcast.47) | data formatting | bytes 4194304 | tf_op jit(solution)/shard_map/concatenate | solution.py:183
  37.3 1.2 copy.22
  38.9 56.7 %all_to_all.20 = bf16[128,32,512]{2,1,0:T(8,128)(2,1)} all-to-all(bf16[128,32,512]{2,1,0:T(8,128)(2,1)S(1)} %bitcast.45), channel_id=1, replica_groups=mesh['sub'=128] {'sub'}, dimensions={0} | all-to-all | bytes 8388608 | tf_op jit(solution)/shard_map/all_to_all | solution.py:191
  95.6 3.4 %broadcast_in_dim.13 = bf16[128,2,4096]{2,1,0:T(2,128)(2,1)} broadcast(bf16[2,4096]{1,0:T(2,128)(2,1)S(1)} %copy-done.4), dimensions={1,2} | broadcast | bytes 2113536 | tf_op jit(solution)/shard_map/broadcast_in_dim | solution.py:174
  99.0 10.9 %all-to-all-start = ((bf16[128,2,4096]{2,1,0:T(2,128)(2,1)}), bf16[128,2,4096]{2,1,0:T(2,128)(2,1)S(1)}, u32[]{:S(2)}, u32[]{:S(2)}) async-start(bf16[128,2,4096]{2,1,0:T(2,128)(2,1)} %broadcast_in_dim.13), calls=%async_computation | async-start | bytes 4194304 | tf_op jit(solution)/shard_map/all_to_all | solution.py:173
  110.0 15.5 %scatter_custom_fusion = s32[4096]{0:T(1024)S(1)} fusion(s32[4096]{0:T(1024)S(1)} %compare_select_fusion, s32[4096]{0:T(1024)S(1)} %iota.7, s32[]{:T(128)} %constant.13.clone.1), kind=kCustom, calls=%fused_computation.22 | custom fusion | bytes 16388 | tf_op jit(solution)/shard_map/scatter | solution.py:196
  125.6 20.2 %gather_fusion = bf16[4096,512]{1,0:T(8,128)(2,1)} fusion(bf16[4096,512]{1,0:T(8,128)(2,1)} %bitcast.43, s32[4096]{0:T(1024)S(1)} %broadcast_clamp_fusion), kind=kCustom, calls=%fused_computation | custom fusion | bytes 8404992 | tf_op jit(solution)/shard_map/jit(_take)/gather | solution.py:198
  145.7 1.3 copy-done.3
  147.1 10.2 %all-to-all-start.2 = ((bf16[128,32,512]{2,1,0:T(8,128)(2,1)}), bf16[128,32,512]{2,1,0:T(8,128)(2,1)}, u32[]{:S(2)}, u32[]{:S(2)}) async-start(bf16[128,32,512]{2,1,0:T(8,128)(2,1)} %bitcast.44), calls=%async_computation.2 | async-start | bytes 8388608 | tf_op jit(solution)/shard_map/all_to_all | solution.py:201
  157.3 4.3 %reshape.39 = bf16[256,4096]{1,0:T(8,128)(2,1)} reshape(bf16[128,2,4096]{2,1,0:T(2,128)(2,1)} %copy-done.3) | data formatting | bytes 4194304 | tf_op jit(solution)/shard_map/reshape | solution.py:175
  161.6 6.8 %convolution_multiply_fusion = f32[256,4096]{1,0:T(8,128)} fusion(bf16[256,4096]{1,0:T(8,128)(2,1)} %get-tuple-element.11, bf16[256,4096]{1,0:T(8,128)(2,1)S(1)} %copy-done.1, bf16[256,4096]{1,0:T(8,128)(2,1)} %reshape.39), kind=kOutput, calls=%fused_computation.2 | convolution fusion | flops 1075445760 | bytes 10485760 | tf_op jit(solution)/shard_map/dot_general | solution.py:210
  168.4 5.9 %reshape.40 = f32[64,2,2,4096]{3,2,1,0:T(2,128)} reshape(f32[256,4096]{1,0:T(8,128)} %convolution_multiply_fusion) | data formatting | bytes 8388608 | tf_op jit(solution)/shard_map/reshape | solution.py:213
  174.3 5.8 %fusion = f32[64,2,4096]{2,1,0:T(2,128)} fusion(pred[]{:T(512)S(6)} %eq.6, f32[64,2,2,4096]{3,2,1,0:T(2,128)} %reshape.40), kind=kLoop, calls=%fused_computation.6 | loop fusion | flops 524288 | bytes 6291457 | tf_op jit(solution)/shard_map/jit(_where)/select_n | solution.py:215
  180.1 1.5 fusion.1
  181.6 22.2 %all-to-all-done.2 = bf16[128,32,512]{2,1,0:T(8,128)(2,1)} async-done(((bf16[128,32,512]{2,1,0:T(8,128)(2,1)}), bf16[128,32,512]{2,1,0:T(8,128)(2,1)}, u32[]{:S(2)}, u32[]{:S(2)}) %all-to-all-start.2) | async-done | bytes 4194336 | tf_op jit(solution)/shard_map/all_to_all | solution.py:201
  203.8 6.5 %copy.26 = bf16[128,32,512]{2,0,1:T(8,128)(2,1)} copy(bf16[128,32,512]{2,1,0:T(8,128)(2,1)} %all-to-all-done.2) | data formatting | bytes 8388608 | tf_op jit(solution)/shard_map/all_to_all | solution.py:201
  210.4 7.4 %reshape.45.refs_4_ = bf16[32,16,4096]{2,1,0:T(8,128)(2,1)} reshape(bf16[32,16,8,512]{3,2,1,0:T(8,128)(2,1)} %bitcast.46) | data formatting | bytes 8388608 | tf_op jit(solution)/shard_map/reshape | solution.py:205
  217.8 4.4 %collective-permute-done = f32[64,2,4096]{2,1,0:T(2,128)S(1)} collective-permute-done((f32[64,2,4096]{2,1,0:T(2,128)}, f32[64,2,4096]{2,1,0:T(2,128)S(1)}, u32[]{:S(2)}, u32[]{:S(2)}) %collective-permute-start) | collective-permute-done | bytes 2097184 | tf_op jit(solution)/shard_map/ppermute | solution.py:218
  222.1 2.8 %add.28 = f32[64,2,4096]{2,1,0:T(2,128)} add(f32[64,2,4096]{2,1,0:T(2,128)S(1)} %fusion.1, f32[64,2,4096]{2,1,0:T(2,128)S(1)} %collective-permute-done) | non-fusion elementwise | flops 524288 | bytes 6291456 | tf_op jit(solution)/shard_map/add | solution.py:218
  225.0 11.7 %all-to-all-start.3 = ((f32[64,2,4096]{2,1,0:T(2,128)}), f32[64,2,4096]{2,1,0:T(2,128)}, u32[]{:S(2)}, u32[]{:S(2)}) async-start(f32[64,2,4096]{2,1,0:T(2,128)} %add.28), calls=%async_computation.3 | async-start | bytes 4194304 | tf_op jit(solution)/shard_map/all_to_all | solution.py:220
  237.2 32.5 %second_round.1 = (f32[4096,256]{1,0:T(8,128)}, f32[4096,256]{1,0:T(8,128)}) custom-call(s32[32]{0:T(128)} %iota.6.refs_0_, s32[256,4]{1,0:T(8,128)} %get-tuple-element.18.refs_1_, bf16[512,4096]{1,0:T(8,128)(2,1)} %refs_2_.3, bf16[512,4096]{1,0:T(8,128)(2,1)} %refs_3_.3, bf16[32,16,4096]{2,1,0:T(8,128)(2,1)} %reshape.45.refs_4_), custom_call_target="tpu_custom_call" | custom-call | flops 19327352832 | bytes 25165824 | tf_op jit(solution)/shard_map/second_round/pallas_call | solution.py:144
  269.7 2.8 %reduce_sum.9 = f32[2,4096]{1,0:T(2,128)} reduce(f32[64,2,4096]{2,1,0:T(2,128)} %all-to-all-done.3, f32[]{:T(128)} %constant.36.clone.1), dimensions={0}, to_apply=%region_1.2 | reduce | flops 516096 | bytes 2129924 | tf_op jit(solution)/shard_map/reduce_sum | solution.py:221
  (20 shorter events, 1.7 us)
Async XLA Ops:
  34.4 2.9 %copy-start.2 = (bf16[256,4096]{1,0:T(8,128)(2,1)S(1)}, bf16[256,4096]{1,0:T(8,128)(2,1)}, u32[]{:S(2)}) copy-start(bf16[256,4096]{1,0:T(8,128)(2,1)} %get-tuple-element.11) | copy-start | bytes 6291460
  38.9 56.7 %copy-start.4 = (bf16[2,4096]{1,0:T(2,128)(2,1)S(1)}, bf16[2,4096]{1,0:T(2,128)(2,1)}, u32[]{:S(2)}) copy-start(bf16[2,4096]{1,0:T(2,128)(2,1)} %param.12) | copy-start | bytes 49156
  99.0 11.0 %copy-start.5 = (s32[4096]{0:T(1024)S(1)}, s32[4096]{0:T(1024)}, u32[]{:S(2)}) copy-start(s32[4096]{0:T(1024)} %param.13) | copy-start | bytes 49156
  99.0 46.7 %all-to-all-start = ((bf16[128,2,4096]{2,1,0:T(2,128)(2,1)}), bf16[128,2,4096]{2,1,0:T(2,128)(2,1)S(1)}, u32[]{:S(2)}, u32[]{:S(2)}) async-start(bf16[128,2,4096]{2,1,0:T(2,128)(2,1)} %broadcast_in_dim.13), calls=%async_computation | async-start | bytes 4194304 | tf_op jit(solution)/shard_map/all_to_all | solution.py:173
  145.7 1.3 copy-start.3
  147.1 56.7 %all-to-all-start.2 = ((bf16[128,32,512]{2,1,0:T(8,128)(2,1)}), bf16[128,32,512]{2,1,0:T(8,128)(2,1)}, u32[]{:S(2)}, u32[]{:S(2)}) async-start(bf16[128,32,512]{2,1,0:T(8,128)(2,1)} %bitcast.44), calls=%async_computation.2 | async-start | bytes 8388608 | tf_op jit(solution)/shard_map/all_to_all | solution.py:201
  157.3 4.3 %copy-start.1 = (bf16[256,4096]{1,0:T(8,128)(2,1)S(1)}, bf16[256,4096]{1,0:T(8,128)(2,1)}, u32[]{:S(2)}) copy-start(bf16[256,4096]{1,0:T(8,128)(2,1)} %get-tuple-element.10) | copy-start | bytes 6291460
  174.3 5.8 %copy-start = (f32[64,2,2,4096]{3,2,1,0:T(2,128)S(1)}, f32[64,2,2,4096]{3,2,1,0:T(2,128)}, u32[]{:S(2)}) copy-start(f32[64,2,2,4096]{3,2,1,0:T(2,128)} %reshape.40) | copy-start | bytes 12582916
  217.8 4.4 %collective-permute-start = (f32[64,2,4096]{2,1,0:T(2,128)}, f32[64,2,4096]{2,1,0:T(2,128)S(1)}, u32[]{:S(2)}, u32[]{:S(2)}) collective-permute-start(f32[64,2,4096]{2,1,0:T(2,128)} %fusion), channel_id=1, source_target_pairs={{0,1},{1,0},{2,3},{3,2},{4,5},{5,4},{6,7},{7,6},{8,9},{9,8},{10,11... | collective-permute-start | bytes 6291464 | tf_op jit(solution)/shard_map/ppermute | solution.py:218
  225.0 44.7 %all-to-all-start.3 = ((f32[64,2,4096]{2,1,0:T(2,128)}), f32[64,2,4096]{2,1,0:T(2,128)}, u32[]{:S(2)}, u32[]{:S(2)}) async-start(f32[64,2,4096]{2,1,0:T(2,128)} %add.28), calls=%async_computation.3 | async-start | bytes 4194304 | tf_op jit(solution)/shard_map/all_to_all | solution.py:220

commit v5 on v4

--- a/solution.py
+++ b/solution.py
@@ -213,9 +213,9 @@
     split = partial.reshape(owners // 2, 2, rows_each, partial.shape[1])
     mine = jnp.where(parity == 0, split[:, 0], split[:, 1])
     other = jnp.where(parity == 0, split[:, 1], split[:, 0])
-    mine, other, landed = lax.optimization_barrier((mine, other, landed))
     pairs = [(k, k ^ 1) for k in range(owners)]
     summed = mine + lax.ppermute(other, "sub", perm=pairs)
+    summed, landed = lax.optimization_barrier((summed, landed))
     same_parity = [list(range(0, owners, 2)), list(range(1, owners, 2))]
     gathered = lax.all_to_all(summed, "sub", 0, 0, tiled=True, axis_index_groups=same_parity)
     prediction = jnp.sum(gathered, axis=0)

time: 276 us -> 254 us (0.920)
  blocking collectives: 56.7 us -> 0 us
  waiting for transfers between devices: 26.6 us -> 53.2 us
  starting transfers between devices: 32.9 us -> 44.6 us
    all_to_all x1 -> x0, blocking collectives: 56.7 us -> none  [per_device(): lax.all_to_all(spread, 'sub', 0, 0, tiled=True)]
    all_to_all x0 -> x1, waiting for transfers between devices: none -> 26.8 us  [per_device(): lax.all_to_all(spread, 'sub', 0, 0, tiled=True)]
    all_to_all x0 -> x1, starting transfers between devices: none -> 10.2 us  [per_device(): lax.all_to_all(spread, 'sub', 0, 0, tiled=True)]
  transfers between devices with their start and end apart: 4 -> 5, of which waited for: 2 -> 3; matrix products, arithmetic and copies ran while one was open for 22% -> 19% of each run, Pallas kernels for 12% -> 26%
where the time goes in v5:
time: 254 us; the launch traced here: 252 us
  local copies, waits for them, and re-layouts  69.3 us (27%)
  Pallas kernels  64.7 us (25%)
  waiting for transfers between devices  53.2 us (21%)
  starting transfers between devices  44.6 us (18%)
  other arithmetic  12.2 us (5%)
  matrix products  6.78 us (3%)
    pallas_call x1, Pallas kernels, second_round(): pl.pallas_call(lambda *refs: second_body(scale_in, scale_out, *refs), out...  32.5 us
    pallas_call x1, Pallas kernels, first_round(): pl.pallas_call(lambda *refs: first_body(scale_in, scale_out, *refs), out_...  32.2 us
    all_to_all x1, waiting for transfers between devices, per_device(): lax.all_to_all(spread, 'sub', 0, 0, tiled=True)  26.8 us
    all_to_all x1, waiting for transfers between devices, per_device(): arrived = lax.all_to_all(forward, 'sub', 0, 0, tiled=True)  22.4 us
    gather x1, local copies, waits for them, and re-layouts, per_device(): jnp.take(held, inverse, axis=0, mode='clip')  20.2 us
    scatter x1, local copies, waits for them, and re-layouts, per_device(): inverse = jnp.zeros((total_groups,), jnp.int32).at[handover].set(jnp.aran...  15.5 us
    all_to_all x1, starting transfers between devices, per_device(): arrived = lax.all_to_all(forward, 'sub', 0, 0, tiled=True)  11.9 us
    all_to_all x1, starting transfers between devices, per_device(): lax.all_to_all(summed, 'sub', 0, 0, tiled=True, axis_index_groups=same_pa...  11.7 us
  transfers between devices with their start and end apart: 5, of which 3 were waited for; matrix products, arithmetic and copies ran while one was open for 19% of the time, Pallas kernels for 26%

profile of v5, /device:TPU:84, one launch (start us, length us, event | category | flops | bytes accessed | tf_op | source)
XLA Modules:
  0.0 251.5 jit_solution(5511449791447014130)
XLA Ops:
  0.6 4.1 %broadcast_in_dim.13 = bf16[128,2,4096]{2,1,0:T(2,128)(2,1)} broadcast(bf16[2,4096]{1,0:T(2,128)(2,1)} %param.12), dimensions={1,2} | broadcast | bytes 2113536 | tf_op jit(solution)/shard_map/broadcast_in_dim | solution.py:174
  4.8 10.4 %all-to-all-start = ((bf16[128,2,4096]{2,1,0:T(2,128)(2,1)}), bf16[128,2,4096]{2,1,0:T(2,128)(2,1)}, u32[]{:S(2)}, u32[]{:S(2)}) async-start(bf16[128,2,4096]{2,1,0:T(2,128)(2,1)} %broadcast_in_dim.13), calls=%async_computation | async-start | bytes 4194304 | tf_op jit(solution)/shard_map/all_to_all | solution.py:173
  15.3 0.8 fusion.21
  16.1 32.2 %first_round.1 = (bf16[256,4096]{1,0:T(8,128)(2,1)}, bf16[256,4096]{1,0:T(8,128)(2,1)}) custom-call(s32[256,4]{1,0:T(8,128)} %get-tuple-element.15.refs_0_, bf16[512,4096]{1,0:T(8,128)(2,1)} %refs_2_.3, bf16[512,4096]{1,0:T(8,128)(2,1)} %refs_3_.3, f32[4096,256]{1,0:T(8,128)} %refs_3_.2, f32[4096,256]{1,0:T(8,128)} %refs_4_.1), custom_call_target="tpu_custom_call" | custom-call | flops 19327352832 | bytes 25165824 | tf_op jit(solution)/shard_map/first_round/pallas_call | solution.py:119
  48.3 2.9 %copy.21 = bf16[32,8,8,512]{3,0,2,1:T(8,128)(2,1)S(1)} copy(bf16[32,8,8,512]{3,1,2,0:T(8,128)(2,1)} %bitcast.50) | data formatting | bytes 4194304 | tf_op jit(solution)/shard_map/concatenate | solution.py:183
  51.2 1.2 copy.22
  52.3 2.4 pad_maximum_fusion
  54.7 10.2 %all-to-all-start.1 = ((bf16[128,32,512]{2,1,0:T(8,128)(2,1)}), bf16[128,32,512]{2,1,0:T(8,128)(2,1)}, u32[]{:S(2)}, u32[]{:S(2)}) async-start(bf16[128,32,512]{2,1,0:T(8,128)(2,1)} %bitcast.48), calls=%async_computation.1 | async-start | bytes 8388608 | tf_op jit(solution)/shard_map/all_to_all | solution.py:191
  65.0 15.5 %scatter_custom_fusion = s32[4096]{0:T(1024)S(1)} fusion(s32[4096]{0:T(1024)S(1)} %compare_select_fusion, s32[4096]{0:T(1024)S(1)} %iota.7, s32[]{:T(128)} %constant.13.clone.1), kind=kCustom, calls=%fused_computation.23 | custom fusion | bytes 16388 | tf_op jit(solution)/shard_map/scatter | solution.py:196
  80.5 4.1 %reshape.39 = bf16[256,4096]{1,0:T(8,128)(2,1)} reshape(bf16[128,2,4096]{2,1,0:T(2,128)(2,1)} %all-to-all-done) | data formatting | bytes 4194304 | tf_op jit(solution)/shard_map/reshape | solution.py:175
  84.7 26.8 %all-to-all-done.1 = bf16[128,32,512]{2,1,0:T(8,128)(2,1)} async-done(((bf16[128,32,512]{2,1,0:T(8,128)(2,1)}), bf16[128,32,512]{2,1,0:T(8,128)(2,1)}, u32[]{:S(2)}, u32[]{:S(2)}) %all-to-all-start.1) | async-done | bytes 4194336 | tf_op jit(solution)/shard_map/all_to_all | solution.py:191
  111.5 20.2 %gather_fusion = bf16[4096,512]{1,0:T(8,128)(2,1)} fusion(bf16[4096,512]{1,0:T(8,128)(2,1)} %bitcast.13, s32[4096]{0:T(1024)S(1)} %broadcast_clamp_fusion), kind=kCustom, calls=%fused_computation | custom fusion | bytes 8404992 | tf_op jit(solution)/shard_map/jit(_take)/gather | solution.py:198
  131.7 11.9 %all-to-all-start.2 = ((bf16[128,32,512]{2,1,0:T(8,128)(2,1)}), bf16[128,32,512]{2,1,0:T(8,128)(2,1)}, u32[]{:S(2)}, u32[]{:S(2)}) async-start(bf16[128,32,512]{2,1,0:T(8,128)(2,1)} %bitcast.47), calls=%async_computation.2 | async-start | bytes 8388608 | tf_op jit(solution)/shard_map/all_to_all | solution.py:201
  143.5 6.8 %convolution_multiply_fusion = f32[256,4096]{1,0:T(8,128)} fusion(bf16[256,4096]{1,0:T(8,128)(2,1)} %get-tuple-element.10, bf16[256,4096]{1,0:T(8,128)(2,1)S(1)} %copy-done.1, bf16[256,4096]{1,0:T(8,128)(2,1)} %reshape.39), kind=kOutput, calls=%fused_computation.2 | convolution fusion | flops 1075445760 | bytes 10485760 | tf_op jit(solution)/shard_map/dot_general | solution.py:210
  150.3 5.9 %reshape.40 = f32[64,2,2,4096]{3,2,1,0:T(2,128)} reshape(f32[256,4096]{1,0:T(8,128)} %convolution_multiply_fusion) | data formatting | bytes 8388608 | tf_op jit(solution)/shard_map/reshape | solution.py:213
  156.2 3.9 %fusion = f32[64,2,4096]{2,1,0:T(2,128)S(1)} fusion(pred[]{:T(512)S(6)} %eq.6, f32[64,2,2,4096]{3,2,1,0:T(2,128)} %reshape.40), kind=kLoop, calls=%fused_computation.6 | loop fusion | flops 524288 | bytes 6291457 | tf_op jit(solution)/shard_map/jit(_where)/select_n | solution.py:215
  160.5 4.0 %collective-permute-done = f32[64,2,4096]{2,1,0:T(2,128)S(1)} collective-permute-done((f32[64,2,4096]{2,1,0:T(2,128)S(1)}, f32[64,2,4096]{2,1,0:T(2,128)S(1)}, u32[]{:S(2)}, u32[]{:S(2)}) %collective-permute-start) | collective-permute-done | bytes 2097184 | tf_op jit(solution)/shard_map/ppermute | solution.py:217
  164.5 3.1 %fusion.2 = f32[64,2,4096]{2,1,0:T(2,128)} fusion(f32[64,2,4096]{2,1,0:T(2,128)S(1)} %collective-permute-done, pred[]{:T(512)S(6)} %eq.6, f32[64,2,2,4096]{3,2,1,0:T(2,128)S(1)} %copy-done), kind=kLoop, calls=%fused_computation.9 | loop fusion | flops 1048576 | bytes 8388609 | tf_op jit(solution)/shard_map/add | solution.py:217
  167.6 22.4 %all-to-all-done.2 = bf16[128,32,512]{2,1,0:T(8,128)(2,1)} async-done(((bf16[128,32,512]{2,1,0:T(8,128)(2,1)}), bf16[128,32,512]{2,1,0:T(8,128)(2,1)}, u32[]{:S(2)}, u32[]{:S(2)}) %all-to-all-start.2) | async-done | bytes 4194336 | tf_op jit(solution)/shard_map/all_to_all | solution.py:201
  190.1 6.5 %copy.26 = bf16[128,32,512]{2,0,1:T(8,128)(2,1)} copy(bf16[128,32,512]{2,1,0:T(8,128)(2,1)} %all-to-all-done.2) | data formatting | bytes 8388608 | tf_op jit(solution)/shard_map/all_to_all | solution.py:201
  196.6 7.4 %reshape.45.refs_4_ = bf16[32,16,4096]{2,1,0:T(8,128)(2,1)} reshape(bf16[32,16,8,512]{3,2,1,0:T(8,128)(2,1)} %bitcast.49) | data formatting | bytes 8388608 | tf_op jit(solution)/shard_map/reshape | solution.py:205
  204.0 11.7 %all-to-all-start.3 = ((f32[64,2,4096]{2,1,0:T(2,128)}), f32[64,2,4096]{2,1,0:T(2,128)}, u32[]{:S(2)}, u32[]{:S(2)}) async-start(f32[64,2,4096]{2,1,0:T(2,128)} %fusion.2), calls=%async_computation.3 | async-start | bytes 4194304 | tf_op jit(solution)/shard_map/all_to_all | solution.py:220
  216.2 32.5 %second_round.1 = (f32[4096,256]{1,0:T(8,128)}, f32[4096,256]{1,0:T(8,128)}) custom-call(s32[32]{0:T(128)} %iota.6.refs_0_, s32[256,4]{1,0:T(8,128)} %get-tuple-element.16.refs_1_, bf16[512,4096]{1,0:T(8,128)(2,1)} %refs_2_.3, bf16[512,4096]{1,0:T(8,128)(2,1)} %refs_3_.3, bf16[32,16,4096]{2,1,0:T(8,128)(2,1)} %reshape.45.refs_4_), custom_call_target="tpu_custom_call" | custom-call | flops 19327352832 | bytes 25165824 | tf_op jit(solution)/shard_map/second_round/pallas_call | solution.py:144
  248.7 2.8 %reduce_sum.9 = f32[2,4096]{1,0:T(2,128)} reduce(f32[64,2,4096]{2,1,0:T(2,128)} %all-to-all-done.3, f32[]{:T(128)} %constant.36.clone.1), dimensions={0}, to_apply=%region_1.2 | reduce | flops 516096 | bytes 2129924 | tf_op jit(solution)/shard_map/reduce_sum | solution.py:221
  (18 shorter events, 1.1 us)
Async XLA Ops:
  4.8 10.4 %copy-start.4 = (s32[8,256]{1,0:T(8,128)S(1)}, s32[8,256]{1,0:T(8,128)}, u32[]{:S(2)}) copy-start(s32[8,256]{1,0:T(8,128)} %param.9) | copy-start | bytes 24580
  4.8 49.9 %all-to-all-start = ((bf16[128,2,4096]{2,1,0:T(2,128)(2,1)}), bf16[128,2,4096]{2,1,0:T(2,128)(2,1)}, u32[]{:S(2)}, u32[]{:S(2)}) async-start(bf16[128,2,4096]{2,1,0:T(2,128)(2,1)} %broadcast_in_dim.13), calls=%async_computation | async-start | bytes 4194304 | tf_op jit(solution)/shard_map/all_to_all | solution.py:173
  48.3 2.9 %copy-start.2 = (bf16[256,4096]{1,0:T(8,128)(2,1)S(1)}, bf16[256,4096]{1,0:T(8,128)(2,1)}, u32[]{:S(2)}) copy-start(bf16[256,4096]{1,0:T(8,128)(2,1)} %get-tuple-element.10) | copy-start | bytes 6291460
  54.7 10.2 %copy-start.3 = (s32[4096]{0:T(1024)S(1)}, s32[4096]{0:T(1024)}, u32[]{:S(2)}) copy-start(s32[4096]{0:T(1024)} %param.13) | copy-start | bytes 49156
  54.7 56.7 %all-to-all-start.1 = ((bf16[128,32,512]{2,1,0:T(8,128)(2,1)}), bf16[128,32,512]{2,1,0:T(8,128)(2,1)}, u32[]{:S(2)}, u32[]{:S(2)}) async-start(bf16[128,32,512]{2,1,0:T(8,128)(2,1)} %bitcast.48), calls=%async_computation.1 | async-start | bytes 8388608 | tf_op jit(solution)/shard_map/all_to_all | solution.py:191
  131.6 11.9 %copy-start.1 = (bf16[256,4096]{1,0:T(8,128)(2,1)S(1)}, bf16[256,4096]{1,0:T(8,128)(2,1)}, u32[]{:S(2)}) copy-start(bf16[256,4096]{1,0:T(8,128)(2,1)} %get-tuple-element.9) | copy-start | bytes 6291460
  131.7 58.4 %all-to-all-start.2 = ((bf16[128,32,512]{2,1,0:T(8,128)(2,1)}), bf16[128,32,512]{2,1,0:T(8,128)(2,1)}, u32[]{:S(2)}, u32[]{:S(2)}) async-start(bf16[128,32,512]{2,1,0:T(8,128)(2,1)} %bitcast.47), calls=%async_computation.2 | async-start | bytes 8388608 | tf_op jit(solution)/shard_map/all_to_all | solution.py:201
  156.2 8.4 %copy-start = (f32[64,2,2,4096]{3,2,1,0:T(2,128)S(1)}, f32[64,2,2,4096]{3,2,1,0:T(2,128)}, u32[]{:S(2)}) copy-start(f32[64,2,2,4096]{3,2,1,0:T(2,128)} %reshape.40) | copy-start | bytes 12582916
  160.1 4.5 %collective-permute-start = (f32[64,2,4096]{2,1,0:T(2,128)S(1)}, f32[64,2,4096]{2,1,0:T(2,128)S(1)}, u32[]{:S(2)}, u32[]{:S(2)}) collective-permute-start(f32[64,2,4096]{2,1,0:T(2,128)S(1)} %fusion), channel_id=1, source_target_pairs={{0,1},{1,0},{2,3},{3,2},{4,5},{5,4},{6,7},{7,6},{8,9},{9,8},{10,11... | collective-permute-start | bytes 6291464 | tf_op jit(solution)/shard_map/ppermute | solution.py:217
  204.0 44.7 %all-to-all-start.3 = ((f32[64,2,4096]{2,1,0:T(2,128)}), f32[64,2,4096]{2,1,0:T(2,128)}, u32[]{:S(2)}, u32[]{:S(2)}) async-start(f32[64,2,4096]{2,1,0:T(2,128)} %fusion.2), calls=%async_computation.3 | async-start | bytes 4194304 | tf_op jit(solution)/shard_map/all_to_all | solution.py:220

commit v6 on v5

--- a/solution.py
+++ b/solution.py
@@ -195,7 +195,7 @@
         .at[handover]
         .set(jnp.arange(total_groups, dtype=jnp.int32))
     )
-    forward = jnp.take(held, inverse, axis=0, mode="clip").reshape(
+    forward = held.at[inverse].get(mode="clip", unique_indices=True).reshape(
         owners, group_count, piece
     )
     arrived = lax.all_to_all(forward, "sub", 0, 0, tiled=True)

time: 254 us -> 254 us (level)
  no operation moved by 1% of the time
where the time goes in v6:
time: 254 us; the launch traced here: 252 us
  local copies, waits for them, and re-layouts  69.3 us (27%)
  Pallas kernels  64.7 us (25%)
  waiting for transfers between devices  53.2 us (21%)
  starting transfers between devices  44.6 us (18%)
  other arithmetic  12.2 us (5%)
  matrix products  6.78 us (3%)
    pallas_call x1, Pallas kernels, second_round(): pl.pallas_call(lambda *refs: second_body(scale_in, scale_out, *refs), out...  32.5 us
    pallas_call x1, Pallas kernels, first_round(): pl.pallas_call(lambda *refs: first_body(scale_in, scale_out, *refs), out_...  32.2 us
    all_to_all x1, waiting for transfers between devices, per_device(): lax.all_to_all(spread, 'sub', 0, 0, tiled=True)  26.8 us
    all_to_all x1, waiting for transfers between devices, per_device(): arrived = lax.all_to_all(forward, 'sub', 0, 0, tiled=True)  22.4 us
    gather x1, local copies, waits for them, and re-layouts, per_device(): held.at[inverse].get(mode='clip', unique_indices=True)  20.2 us
    scatter x1, local copies, waits for them, and re-layouts, per_device(): inverse = jnp.zeros((total_groups,), jnp.int32).at[handover].set(jnp.aran...  15.5 us
    all_to_all x1, starting transfers between devices, per_device(): arrived = lax.all_to_all(forward, 'sub', 0, 0, tiled=True)  11.9 us
    all_to_all x1, starting transfers between devices, per_device(): lax.all_to_all(summed, 'sub', 0, 0, tiled=True, axis_index_groups=same_pa...  11.7 us
  transfers between devices with their start and end apart: 5, of which 3 were waited for; matrix products, arithmetic and copies ran while one was open for 19% of the time, Pallas kernels for 26%

profile of v6, /device:TPU:84, one launch (start us, length us, event | category | flops | bytes accessed | tf_op | source)
XLA Modules:
  0.0 251.5 jit_solution(12249319560137387456)
XLA Ops:
  0.6 4.1 %broadcast_in_dim.12 = bf16[128,2,4096]{2,1,0:T(2,128)(2,1)} broadcast(bf16[2,4096]{1,0:T(2,128)(2,1)} %param.12), dimensions={1,2} | broadcast | bytes 2113536 | tf_op jit(solution)/shard_map/broadcast_in_dim | solution.py:174
  4.8 10.4 %all-to-all-start = ((bf16[128,2,4096]{2,1,0:T(2,128)(2,1)}), bf16[128,2,4096]{2,1,0:T(2,128)(2,1)}, u32[]{:S(2)}, u32[]{:S(2)}) async-start(bf16[128,2,4096]{2,1,0:T(2,128)(2,1)} %broadcast_in_dim.12), calls=%async_computation | async-start | bytes 4194304 | tf_op jit(solution)/shard_map/all_to_all | solution.py:173
  15.3 0.8 fusion.22
  16.1 32.2 %first_round.1 = (bf16[256,4096]{1,0:T(8,128)(2,1)}, bf16[256,4096]{1,0:T(8,128)(2,1)}) custom-call(s32[256,4]{1,0:T(8,128)} %get-tuple-element.15.refs_0_, bf16[512,4096]{1,0:T(8,128)(2,1)} %refs_2_.3, bf16[512,4096]{1,0:T(8,128)(2,1)} %refs_3_.3, f32[4096,256]{1,0:T(8,128)} %refs_3_.2, f32[4096,256]{1,0:T(8,128)} %refs_4_.1), custom_call_target="tpu_custom_call" | custom-call | flops 19327352832 | bytes 25165824 | tf_op jit(solution)/shard_map/first_round/pallas_call | solution.py:119
  48.3 2.9 %copy.21 = bf16[32,8,8,512]{3,0,2,1:T(8,128)(2,1)S(1)} copy(bf16[32,8,8,512]{3,1,2,0:T(8,128)(2,1)} %bitcast.50) | data formatting | bytes 4194304 | tf_op jit(solution)/shard_map/concatenate | solution.py:183
  51.2 1.2 copy.22
  52.3 2.4 pad_maximum_fusion
  54.7 10.2 %all-to-all-start.1 = ((bf16[128,32,512]{2,1,0:T(8,128)(2,1)}), bf16[128,32,512]{2,1,0:T(8,128)(2,1)}, u32[]{:S(2)}, u32[]{:S(2)}) async-start(bf16[128,32,512]{2,1,0:T(8,128)(2,1)} %bitcast.48), calls=%async_computation.1 | async-start | bytes 8388608 | tf_op jit(solution)/shard_map/all_to_all | solution.py:191
  65.0 15.5 %scatter_custom_fusion = s32[4096]{0:T(1024)S(1)} fusion(s32[4096]{0:T(1024)S(1)} %compare_select_fusion.1, s32[4096]{0:T(1024)S(1)} %iota.7, s32[]{:T(128)} %constant.13.clone.1), kind=kCustom, calls=%fused_computation.24 | custom fusion | bytes 16388 | tf_op jit(solution)/shard_map/scatter | solution.py:196
  80.5 4.1 %reshape.39 = bf16[256,4096]{1,0:T(8,128)(2,1)} reshape(bf16[128,2,4096]{2,1,0:T(2,128)(2,1)} %all-to-all-done) | data formatting | bytes 4194304 | tf_op jit(solution)/shard_map/reshape | solution.py:175
  84.7 26.8 %all-to-all-done.1 = bf16[128,32,512]{2,1,0:T(8,128)(2,1)} async-done(((bf16[128,32,512]{2,1,0:T(8,128)(2,1)}), bf16[128,32,512]{2,1,0:T(8,128)(2,1)}, u32[]{:S(2)}, u32[]{:S(2)}) %all-to-all-start.1) | async-done | bytes 4194336 | tf_op jit(solution)/shard_map/all_to_all | solution.py:191
  111.5 20.2 %gather_fusion = bf16[4096,512]{1,0:T(8,128)(2,1)} fusion(bf16[4096,512]{1,0:T(8,128)(2,1)} %bitcast.13, s32[4096]{0:T(1024)S(1)} %fusion.14), kind=kCustom, calls=%fused_computation | custom fusion | bytes 8404992 | tf_op jit(solution)/shard_map/gather | solution.py:198
  131.7 11.9 %all-to-all-start.2 = ((bf16[128,32,512]{2,1,0:T(8,128)(2,1)}), bf16[128,32,512]{2,1,0:T(8,128)(2,1)}, u32[]{:S(2)}, u32[]{:S(2)}) async-start(bf16[128,32,512]{2,1,0:T(8,128)(2,1)} %bitcast.47), calls=%async_computation.2 | async-start | bytes 8388608 | tf_op jit(solution)/shard_map/all_to_all | solution.py:201
  143.5 6.8 %convolution_multiply_fusion = f32[256,4096]{1,0:T(8,128)} fusion(bf16[256,4096]{1,0:T(8,128)(2,1)} %get-tuple-element.10, bf16[256,4096]{1,0:T(8,128)(2,1)S(1)} %copy-done.1, bf16[256,4096]{1,0:T(8,128)(2,1)} %reshape.39), kind=kOutput, calls=%fused_computation.2 | convolution fusion | flops 1075445760 | bytes 10485760 | tf_op jit(solution)/shard_map/dot_general | solution.py:210
  150.3 5.9 %reshape.40 = f32[64,2,2,4096]{3,2,1,0:T(2,128)} reshape(f32[256,4096]{1,0:T(8,128)} %convolution_multiply_fusion) | data formatting | bytes 8388608 | tf_op jit(solution)/shard_map/reshape | solution.py:213
  156.2 3.9 %fusion = f32[64,2,4096]{2,1,0:T(2,128)S(1)} fusion(pred[]{:T(512)S(6)} %eq.6, f32[64,2,2,4096]{3,2,1,0:T(2,128)} %reshape.40), kind=kLoop, calls=%fused_computation.6 | loop fusion | flops 524288 | bytes 6291457 | tf_op jit(solution)/shard_map/jit(_where)/select_n | solution.py:215
  160.5 4.0 %collective-permute-done = f32[64,2,4096]{2,1,0:T(2,128)S(1)} collective-permute-done((f32[64,2,4096]{2,1,0:T(2,128)S(1)}, f32[64,2,4096]{2,1,0:T(2,128)S(1)}, u32[]{:S(2)}, u32[]{:S(2)}) %collective-permute-start) | collective-permute-done | bytes 2097184 | tf_op jit(solution)/shard_map/ppermute | solution.py:217
  164.5 3.1 %fusion.2 = f32[64,2,4096]{2,1,0:T(2,128)} fusion(f32[64,2,4096]{2,1,0:T(2,128)S(1)} %collective-permute-done, pred[]{:T(512)S(6)} %eq.6, f32[64,2,2,4096]{3,2,1,0:T(2,128)S(1)} %copy-done), kind=kLoop, calls=%fused_computation.9 | loop fusion | flops 1048576 | bytes 8388609 | tf_op jit(solution)/shard_map/add | solution.py:217
  167.6 22.4 %all-to-all-done.2 = bf16[128,32,512]{2,1,0:T(8,128)(2,1)} async-done(((bf16[128,32,512]{2,1,0:T(8,128)(2,1)}), bf16[128,32,512]{2,1,0:T(8,128)(2,1)}, u32[]{:S(2)}, u32[]{:S(2)}) %all-to-all-start.2) | async-done | bytes 4194336 | tf_op jit(solution)/shard_map/all_to_all | solution.py:201
  190.1 6.5 %copy.26 = bf16[128,32,512]{2,0,1:T(8,128)(2,1)} copy(bf16[128,32,512]{2,1,0:T(8,128)(2,1)} %all-to-all-done.2) | data formatting | bytes 8388608 | tf_op jit(solution)/shard_map/all_to_all | solution.py:201
  196.6 7.4 %reshape.45.refs_4_ = bf16[32,16,4096]{2,1,0:T(8,128)(2,1)} reshape(bf16[32,16,8,512]{3,2,1,0:T(8,128)(2,1)} %bitcast.49) | data formatting | bytes 8388608 | tf_op jit(solution)/shard_map/reshape | solution.py:205
  204.0 11.7 %all-to-all-start.3 = ((f32[64,2,4096]{2,1,0:T(2,128)}), f32[64,2,4096]{2,1,0:T(2,128)}, u32[]{:S(2)}, u32[]{:S(2)}) async-start(f32[64,2,4096]{2,1,0:T(2,128)} %fusion.2), calls=%async_computation.3 | async-start | bytes 4194304 | tf_op jit(solution)/shard_map/all_to_all | solution.py:220
  216.2 32.5 %second_round.1 = (f32[4096,256]{1,0:T(8,128)}, f32[4096,256]{1,0:T(8,128)}) custom-call(s32[32]{0:T(128)} %iota.6.refs_0_, s32[256,4]{1,0:T(8,128)} %get-tuple-element.16.refs_1_, bf16[512,4096]{1,0:T(8,128)(2,1)} %refs_2_.3, bf16[512,4096]{1,0:T(8,128)(2,1)} %refs_3_.3, bf16[32,16,4096]{2,1,0:T(8,128)(2,1)} %reshape.45.refs_4_), custom_call_target="tpu_custom_call" | custom-call | flops 19327352832 | bytes 25165824 | tf_op jit(solution)/shard_map/second_round/pallas_call | solution.py:144
  248.7 2.8 %reduce_sum.9 = f32[2,4096]{1,0:T(2,128)} reduce(f32[64,2,4096]{2,1,0:T(2,128)} %all-to-all-done.3, f32[]{:T(128)} %constant.36.clone.1), dimensions={0}, to_apply=%region_1.2 | reduce | flops 516096 | bytes 2129924 | tf_op jit(solution)/shard_map/reduce_sum | solution.py:221
  (18 shorter events, 1.1 us)
Async XLA Ops:
  4.8 10.4 %copy-start.4 = (s32[8,256]{1,0:T(8,128)S(1)}, s32[8,256]{1,0:T(8,128)}, u32[]{:S(2)}) copy-start(s32[8,256]{1,0:T(8,128)} %param.9) | copy-start | bytes 24580
  4.8 49.9 %all-to-all-start = ((bf16[128,2,4096]{2,1,0:T(2,128)(2,1)}), bf16[128,2,4096]{2,1,0:T(2,128)(2,1)}, u32[]{:S(2)}, u32[]{:S(2)}) async-start(bf16[128,2,4096]{2,1,0:T(2,128)(2,1)} %broadcast_in_dim.12), calls=%async_computation | async-start | bytes 4194304 | tf_op jit(solution)/shard_map/all_to_all | solution.py:173
  48.3 2.9 %copy-start.2 = (bf16[256,4096]{1,0:T(8,128)(2,1)S(1)}, bf16[256,4096]{1,0:T(8,128)(2,1)}, u32[]{:S(2)}) copy-start(bf16[256,4096]{1,0:T(8,128)(2,1)} %get-tuple-element.10) | copy-start | bytes 6291460
  54.7 10.2 %copy-start.3 = (s32[4096]{0:T(1024)S(1)}, s32[4096]{0:T(1024)}, u32[]{:S(2)}) copy-start(s32[4096]{0:T(1024)} %param.13) | copy-start | bytes 49156
  54.7 56.7 %all-to-all-start.1 = ((bf16[128,32,512]{2,1,0:T(8,128)(2,1)}), bf16[128,32,512]{2,1,0:T(8,128)(2,1)}, u32[]{:S(2)}, u32[]{:S(2)}) async-start(bf16[128,32,512]{2,1,0:T(8,128)(2,1)} %bitcast.48), calls=%async_computation.1 | async-start | bytes 8388608 | tf_op jit(solution)/shard_map/all_to_all | solution.py:191
  131.6 11.9 %copy-start.1 = (bf16[256,4096]{1,0:T(8,128)(2,1)S(1)}, bf16[256,4096]{1,0:T(8,128)(2,1)}, u32[]{:S(2)}) copy-start(bf16[256,4096]{1,0:T(8,128)(2,1)} %get-tuple-element.9) | copy-start | bytes 6291460
  131.7 58.4 %all-to-all-start.2 = ((bf16[128,32,512]{2,1,0:T(8,128)(2,1)}), bf16[128,32,512]{2,1,0:T(8,128)(2,1)}, u32[]{:S(2)}, u32[]{:S(2)}) async-start(bf16[128,32,512]{2,1,0:T(8,128)(2,1)} %bitcast.47), calls=%async_computation.2 | async-start | bytes 8388608 | tf_op jit(solution)/shard_map/all_to_all | solution.py:201
  156.2 8.4 %copy-start = (f32[64,2,2,4096]{3,2,1,0:T(2,128)S(1)}, f32[64,2,2,4096]{3,2,1,0:T(2,128)}, u32[]{:S(2)}) copy-start(f32[64,2,2,4096]{3,2,1,0:T(2,128)} %reshape.40) | copy-start | bytes 12582916
  160.1 4.5 %collective-permute-start = (f32[64,2,4096]{2,1,0:T(2,128)S(1)}, f32[64,2,4096]{2,1,0:T(2,128)S(1)}, u32[]{:S(2)}, u32[]{:S(2)}) collective-permute-start(f32[64,2,4096]{2,1,0:T(2,128)S(1)} %fusion), channel_id=1, source_target_pairs={{0,1},{1,0},{2,3},{3,2},{4,5},{5,4},{6,7},{7,6},{8,9},{9,8},{10,11... | collective-permute-start | bytes 6291464 | tf_op jit(solution)/shard_map/ppermute | solution.py:217
  204.0 44.7 %all-to-all-start.3 = ((f32[64,2,4096]{2,1,0:T(2,128)}), f32[64,2,4096]{2,1,0:T(2,128)}, u32[]{:S(2)}, u32[]{:S(2)}) async-start(f32[64,2,4096]{2,1,0:T(2,128)} %fusion.2), calls=%async_computation.3 | async-start | bytes 4194304 | tf_op jit(solution)/shard_map/all_to_all | solution.py:220
